TPU v7x, 32 devices: a whole 2x2x4 slice. The times are simulated.
32 devices in a mesh: rows: 8 (over z, x), cols: 4 (over y, core).
Axes of the slice: x: 2, y: 2, z: 4, core: 2. Of those that a mesh axis runs over, the one named last changes fastest.
Arguments:
- vectors: bfloat16 [64, 131072], P('cols', 'rows'), may hold values from -110 to 110
- tile_vals: bfloat16 [1536, 256, 256], P('rows'), may hold values from -0.21875 to 0.21875
- tile_row: int32 [8, 192], P('rows'), may hold values from 0 to 63
- tile_src: int32 [8, 192], P('rows'), may hold values from 0 to 191, each once within a row
- send_list: int32 [64, 16], P('rows'), may hold values from 0 to 63
- ritz_matrix: bfloat16 [64, 64], P(None, 'cols'), may hold values from -0.75 to 0.75
Outputs:
- rotated: bfloat16 [64, 131072], P('cols', 'rows')
- gram_matrix: float32 [64, 64], P('cols')
- projected: float32 [64, 64], P('cols')
Inputs may be any that keep to these rules, and one draw needn't show every extreme that they name: Each row of tile_src holds every number once, so that each own or received block is read by exactly one tile.
All inputs are finite; a program needn't handle non-finite values.
Results may differ from a plain program's by a relative error of at most 0.0062.
Values may be sent and summed in bfloat16 or wider, within the bound.
No kernel may reach another device: no remote copies, remote signals or barrier semaphores. Data moves between devices by JAX's collectives and lax.ppermute only.
A program may use at most 128 MiB of HBM per device.

v0:
```python
import jax
import jax.numpy as jnp
from jax import lax
from jax.sharding import PartitionSpec as P


def tile_products(sources, tile_block, row_ids, src_ids, nblocks):
    chosen = jnp.take(sources, src_ids, axis=1)
    products = jnp.einsum("ktc,trc->ktr", chosen, tile_block, preferred_element_type=jnp.float32)
    onehot = (row_ids[None, :] == jnp.arange(nblocks, dtype=jnp.int32)[:, None]).astype(jnp.float32)
    summed = jnp.einsum("bt,ktr->kbr", onehot, products, precision=lax.Precision.HIGHEST)
    return summed.reshape(summed.shape[0], -1)


def apply_operator(vectors, tile_vals, tile_row, tile_src, send_list):
    columns, length = vectors.shape
    tile_side = tile_vals.shape[1]
    nblocks = length // tile_side
    blocked = vectors.reshape(columns, nblocks, tile_side)
    outgoing = jnp.take(blocked, send_list.reshape(-1), axis=1)
    incoming = lax.all_to_all(outgoing, "rows", split_axis=1, concat_axis=1, tiled=True)
    row_ids = tile_row.reshape(-1)
    src_ids = tile_src.reshape(-1)
    sources = jnp.concatenate([blocked, incoming], axis=1)
    return tile_products(sources, tile_vals, row_ids, src_ids, nblocks)


def contract_nodes(left_side, right_side):
    return lax.dot_general(
        left_side, right_side, (((1,), (1,)), ((), ())), preferred_element_type=jnp.float32
    )


def body(vectors, tile_vals, tile_row, tile_src, send_list, ritz_matrix):
    first_pass = apply_operator(vectors, tile_vals, tile_row, tile_src, send_list).astype(
        jnp.bfloat16
    )
    second = apply_operator(first_pass, tile_vals, tile_row, tile_src, send_list)
    filtered = (2.0 * second - vectors.astype(jnp.float32)).astype(jnp.bfloat16)
    total_nodes = vectors.shape[1] * lax.axis_size("rows")
    operated = apply_operator(filtered, tile_vals, tile_row, tile_src, send_list).astype(
        jnp.bfloat16
    )
    portion = lax.all_gather(filtered, "cols", axis=0, tiled=True)
    gram_piece = contract_nodes(filtered, portion)
    proj_piece = contract_nodes(operated, portion)
    turned = lax.dot_general(
        ritz_matrix, portion, (((0,), (0,)), ((), ())), preferred_element_type=jnp.float32
    )
    gram_total, proj_total = lax.psum((gram_piece, proj_piece), "rows")
    gram_matrix = gram_total / total_nodes
    projected = proj_total / total_nodes
    rotated = turned.astype(jnp.bfloat16)
    return (rotated, gram_matrix, projected)


def solution(mesh):
    return jax.shard_map(
        body,
        mesh=mesh,
        in_specs=(
            P("cols", "rows"),
            P("rows", None, None),
            P("rows", None),
            P("rows", None),
            P("rows", None),
            P(None, "cols"),
        ),
        out_specs=(P("cols", "rows"), P("cols", None), P("cols", None)),
        check_vma=False,
    )
```

profile of v0, /device:TPU:0, one launch (start us, length us, event | category | flops | bytes accessed | tf_op | source)
XLA Modules:
  0.0 207.6 jit_solution(13215640300237485455)
XLA Ops:
  7.2 0.8 reshape.40
  8.0 1.1 copy.41
  9.1 0.6 gather_fusion
  9.7 1.2 select_bitcast_fusion.2
  10.9 7.4 %all-to-all-start = ((bf16[16,128,256]{2,0,1:T(8,128)(2,1)}), bf16[16,128,256]{2,0,1:T(8,128)(2,1)S(1)}, u32[]{:S(2)}, u32[]{:S(2)}) async-start(bf16[16,128,256]{2,0,1:T(8,128)(2,1)} %select_bitcast_fusion.2), calls=%async_computation | async-start | bytes 2097152 | tf_op jit(solution)/shard_map/all_to_all | solution.py:21
  18.4 25.7 %all-to-all-done = bf16[16,128,256]{2,0,1:T(8,128)(2,1)S(1)} async-done(((bf16[16,128,256]{2,0,1:T(8,128)(2,1)}), bf16[16,128,256]{2,0,1:T(8,128)(2,1)S(1)}, u32[]{:S(2)}, u32[]{:S(2)}) %all-to-all-start) | async-done | bytes 1048608 | tf_op jit(solution)/shard_map/all_to_all | solution.py:21
  44.2 2.0 gather_fusion.1
  46.3 12.0 %convolution_bitcast_fusion.2 = f32[16,192,256]{2,0,1:T(8,128)S(1)} fusion(bf16[192,256,256]{2,1,0:T(8,128)(2,1)} %param.11, bf16[192,16,256]{2,1,0:T(8,128)(2,1)} %gather_fusion.1, pred[192]{0:T(512)(128)(4,1)S(1)} %compare_and_fusion), kind=kOutput, calls=%fused_computation.16 | convolution fusion | flops 403439616 | bytes 29884608 | tf_op jit(solution)/shard_map/ktc,trc->ktr/dot_general | solution.py:9
  58.3 3.2 %fusion.25 = bf16[16,64,256]{2,1,0:T(8,128)(2,1)S(1)} fusion(f32[16,192,256]{2,0,1:T(8,128)S(1)} %convolution_bitcast_fusion.2, s32[192]{0:T(256)S(1)} %bitcast.65), kind=kOutput, calls=%fused_computation.32 | convolution fusion | flops 604254208 | bytes 3670784 | tf_op jit(solution)/shard_map/bt,ktr->kbr/dot_general | solution.py:11
  62.6 29.3 %all_to_all.15 = bf16[16,128,256]{2,0,1:T(8,128)(2,1)S(1)} all-to-all(bf16[16,128,256]{2,0,1:T(8,128)(2,1)S(1)} %select_bitcast_fusion.1), channel_id=1, replica_groups=mesh['rows'=8,'cols'=4] {'rows'}, dimensions={1} | all-to-all | bytes 2097152 | tf_op jit(solution)/shard_map/all_to_all | solution.py:21
  92.1 2.0 gather_fusion.3
  94.1 12.0 %convolution_bitcast_fusion.1 = f32[16,192,256]{2,0,1:T(8,128)S(1)} fusion(bf16[192,256,256]{2,1,0:T(8,128)(2,1)} %param.11, bf16[192,16,256]{2,1,0:T(8,128)(2,1)} %gather_fusion.3, pred[192]{0:T(512)(128)(4,1)S(1)} %compare_and_fusion), kind=kOutput, calls=%fused_computation.15 | convolution fusion | flops 403439616 | bytes 29884608 | tf_op jit(solution)/shard_map/ktc,trc->ktr/dot_general | solution.py:9
  106.1 3.2 %fusion.16 = f32[16,256,64]{1,2,0:T(8,128)S(1)} fusion(f32[16,192,256]{2,0,1:T(8,128)S(1)} %convolution_bitcast_fusion.1, s32[192]{0:T(256)S(1)} %bitcast.66), kind=kOutput, calls=%fused_computation.29 | convolution fusion | flops 604254208 | bytes 4195072 | tf_op jit(solution)/shard_map/bt,ktr->kbr/dot_general | solution.py:11
  111.2 1.2 select_bitcast_fusion
  112.4 4.2 %all-to-all-start.2 = ((bf16[16,128,256]{2,0,1:T(8,128)(2,1)}), bf16[16,128,256]{2,0,1:T(8,128)(2,1)}, u32[]{:S(2)}, u32[]{:S(2)}) async-start(bf16[16,128,256]{2,0,1:T(8,128)(2,1)} %select_bitcast_fusion), calls=%async_computation.2 | async-start | bytes 2097152 | tf_op jit(solution)/shard_map/all_to_all | solution.py:21
  117.4 24.4 %all-to-all-done.2 = bf16[16,128,256]{2,0,1:T(8,128)(2,1)} async-done(((bf16[16,128,256]{2,0,1:T(8,128)(2,1)}), bf16[16,128,256]{2,0,1:T(8,128)(2,1)}, u32[]{:S(2)}, u32[]{:S(2)}) %all-to-all-start.2) | async-done | bytes 1048608 | tf_op jit(solution)/shard_map/all_to_all | solution.py:21
  141.8 1.4 pad_maximum_fusion.2
  143.2 2.0 gather_fusion.5
  145.2 12.0 %convolution_bitcast_fusion = f32[16,192,256]{2,0,1:T(8,128)S(1)} fusion(bf16[192,256,256]{2,1,0:T(8,128)(2,1)} %param.11, bf16[192,16,256]{2,1,0:T(8,128)(2,1)} %gather_fusion.5, pred[192]{0:T(512)(128)(4,1)S(1)} %compare_and_fusion), kind=kOutput, calls=%fused_computation.14 | convolution fusion | flops 403439616 | bytes 29884608 | tf_op jit(solution)/shard_map/ktc,trc->ktr/dot_general | solution.py:9
  157.2 3.2 %fusion.22 = bf16[16,256,64]{1,2,0:T(8,128)(2,1)S(1)} fusion(f32[16,192,256]{2,0,1:T(8,128)S(1)} %convolution_bitcast_fusion, s32[192]{0:T(256)S(1)} %bitcast.67), kind=kOutput, calls=%fused_computation.31 | convolution fusion | flops 604254208 | bytes 3670784 | tf_op jit(solution)/shard_map/bt,ktr->kbr/dot_general | solution.py:11
  160.7 2.5 %fusion.41 = f32[16,64]{1,0:T(8,128)S(1)} fusion(bf16[16,16384]{1,0:T(8,128)(2,1)} %copy-done.2, bf16[64,16384]{1,0:T(8,128)(2,1)} %all-gather.2.cloned.1.call-done), kind=kOutput, calls=%fused_computation.58 | convolution fusion | flops 33554432 | bytes 2625536 | tf_op jit(solution)/shard_map/dot_general | solution.py:29
  163.3 0.7 fusion.42
  163.9 35.0 %all-reduce = (f32[16,64]{1,0:T(8,128)S(1)}, f32[16,64]{1,0:T(8,128)S(1)}) all-reduce(f32[16,64]{1,0:T(8,128)S(1)} %fusion.41, f32[16,64]{1,0:T(8,128)S(1)} %fusion.42), channel_id=1, replica_groups=mesh['rows'=8,'cols'=4] {'rows'}, use_global_device_ids=true, to_apply=%region_0.3 | all-reduce | flops 2048 | bytes 16384 | tf_op jit(solution)/shard_map/psum | solution.py:50
  199.5 1.2 fusion
  (32 shorter events, 5.0 us)
Async XLA Ops:
  7.2 192.4 %copy-start = (bf16[64,16]{0,1:T(8,128)(2,1)S(1)}, bf16[64,16]{0,1:T(8,128)(2,1)}, u32[]{:S(2)}) copy-start(bf16[64,16]{0,1:T(8,128)(2,1)} %param.15) | copy-start | bytes 6148
  10.9 7.4 %copy-start.5 = (s32[1,192]{1,0:T(1,128)S(1)}, s32[1,192]{1,0:T(1,128)}, u32[]{:S(2)}) copy-start(s32[1,192]{1,0:T(1,128)} %param.13) | copy-start | bytes 2308
  10.9 33.2 %all-to-all-start = ((bf16[16,128,256]{2,0,1:T(8,128)(2,1)}), bf16[16,128,256]{2,0,1:T(8,128)(2,1)S(1)}, u32[]{:S(2)}, u32[]{:S(2)}) async-start(bf16[16,128,256]{2,0,1:T(8,128)(2,1)} %select_bitcast_fusion.2), calls=%async_computation | async-start | bytes 2097152 | tf_op jit(solution)/shard_map/all_to_all | solution.py:21
  46.3 12.1 %copy-start.4 = (s32[1,192]{1,0:T(1,128)S(1)}, s32[1,192]{1,0:T(1,128)}, u32[]{:S(2)}) copy-start(s32[1,192]{1,0:T(1,128)} %param.12) | copy-start | bytes 2308
  109.3 1.0 copy-start.3
  110.4 0.8 copy-start.2
  112.4 29.4 %all-to-all-start.2 = ((bf16[16,128,256]{2,0,1:T(8,128)(2,1)}), bf16[16,128,256]{2,0,1:T(8,128)(2,1)}, u32[]{:S(2)}, u32[]{:S(2)}) async-start(bf16[16,128,256]{2,0,1:T(8,128)(2,1)} %select_bitcast_fusion), calls=%async_computation.2 | async-start | bytes 2097152 | tf_op jit(solution)/shard_map/all_to_all | solution.py:21
  116.7 44.0 %all-gather.2.cloned.1.call-start = ((), (), s32[]{:S(2)}) async-start(), calls=%async_computation.3 | async-start | bytes 2621440 | tf_op jit(solution)/shard_map/all_gather | solution.py:44
  160.7 2.6 %copy-start.1 = (bf16[64,16384]{1,0:T(8,128)(2,1)S(1)}, bf16[64,16384]{1,0:T(8,128)(2,1)}, u32[]{:S(2)}) copy-start(bf16[64,16384]{1,0:T(8,128)(2,1)} %all-gather.2.cloned.1.call-done) | copy-start | bytes 6291460
Sparse Core Ops, SparseCore 0:
  119.6 23.8 all-gather.1
where the time goes:
time: 208 us
  blocking collectives  64.2 us (31%)
  waiting for transfers between devices  50.6 us (24%)
  matrix products  50 us (24%)
  between operations  14.2 us (7%)
  starting transfers between devices  11.9 us (6%)
  local copies, waits for them, and re-layouts  11.7 us (6%)
  other arithmetic  4.96 us (2%)
    all_to_all x2, waiting for transfers between devices, apply_operator(): lax.all_to_all(outgoing, 'rows', split_axis=1, concat_axis=1, tiled=True)  50.1 us
    dot_general x3, matrix products, tile_products(): jnp.einsum('ktc,trc->ktr', chosen, tile_block, preferred_element_type=jnp...  36.1 us
    psum x1, blocking collectives, body(): gram_total, proj_total = lax.psum((gram_piece, proj_piece), 'rows')  35 us
    all_to_all x1, blocking collectives, apply_operator(): lax.all_to_all(outgoing, 'rows', split_axis=1, concat_axis=1, tiled=True)  29.3 us
    all_to_all x2, starting transfers between devices, apply_operator(): lax.all_to_all(outgoing, 'rows', split_axis=1, concat_axis=1, tiled=True)  11.6 us
    dot_general x3, matrix products, tile_products(): jnp.einsum('bt,ktr->kbr', onehot, products, precision=lax.Precision.HIGHEST)  9.49 us
    gather x3, local copies, waits for them, and re-layouts, tile_products(): chosen = jnp.take(sources, src_ids, axis=1)  6.1 us
  transfers between devices with their start and end apart: 3, of which 2 were waited for; matrix products, arithmetic and copies ran while one was open for 9% of the time, Pallas kernels for 0%

commit v1 on v0

--- a/solution.py
+++ b/solution.py
@@ -12,16 +12,33 @@
     return summed.reshape(summed.shape[0], -1)
 
 
-def apply_operator(vectors, tile_vals, tile_row, tile_src, send_list):
+def remap_sources(tile_src, nblocks, slot, nrows):
+    me = lax.axis_index("rows")
+    src = tile_src.reshape(-1)
+    peer = (src - nblocks) // slot
+    shift = (me - peer) % nrows
+    moved = nblocks + shift * slot + (src - nblocks) % slot
+    return jnp.where(src < nblocks, src, moved)
+
+
+def apply_operator(vectors, tile_vals, tile_row, src_ids, send_list):
     columns, length = vectors.shape
     tile_side = tile_vals.shape[1]
     nblocks = length // tile_side
+    nrows = send_list.shape[0]
+    me = lax.axis_index("rows")
     blocked = vectors.reshape(columns, nblocks, tile_side)
-    outgoing = jnp.take(blocked, send_list.reshape(-1), axis=1)
-    incoming = lax.all_to_all(outgoing, "rows", split_axis=1, concat_axis=1, tiled=True)
+    pieces = []
+    for shift in range(nrows):
+        dest = (me + shift) % nrows
+        wanted = lax.dynamic_index_in_dim(send_list, dest, 0, keepdims=False)
+        chunk = jnp.take(blocked, wanted, axis=1)
+        if shift:
+            pairs = [(i, (i + shift) % nrows) for i in range(nrows)]
+            chunk = lax.ppermute(chunk, "rows", pairs)
+        pieces.append(chunk)
     row_ids = tile_row.reshape(-1)
-    src_ids = tile_src.reshape(-1)
-    sources = jnp.concatenate([blocked, incoming], axis=1)
+    sources = jnp.concatenate([blocked] + pieces, axis=1)
     return tile_products(sources, tile_vals, row_ids, src_ids, nblocks)
 
 
@@ -31,25 +48,66 @@
     )
 
 
+def tree_sum_rows(value, nrows):
+    step = 1
+    while step < nrows:
+        pairs = [(i, i ^ step) for i in range(nrows)]
+        value = value + lax.ppermute(value, "rows", pairs)
+        step *= 2
+    return value
+
+
+def gather_cols(piece, ncols):
+    half = 2 if ncols % 2 == 0 else 1
+    outer = ncols // half
+    parts = [piece]
+    for shift in range(1, outer):
+        pairs = [(i, (i + shift * half) % ncols) for i in range(ncols)]
+        parts.append(lax.ppermute(piece, "cols", pairs))
+    group = jnp.stack(parts)
+    if half == 2:
+        pairs = [(i, i ^ 1) for i in range(ncols)]
+        other = lax.ppermute(group, "cols", pairs)
+        me = lax.axis_index("cols")
+        low = me % 2 == 0
+        group = jnp.where(low, jnp.stack([group, other], 1), jnp.stack([other, group], 1))
+        group = group.reshape((outer * half,) + piece.shape)
+    else:
+        group = group.reshape((outer,) + piece.shape)
+    me = lax.axis_index("cols")
+    m = jnp.arange(ncols)
+    outer_of = (me // half + m // half) % outer
+    absolute = outer_of * half + m % half
+    order = jnp.zeros((ncols,), jnp.int32).at[absolute].set(m.astype(jnp.int32))
+    group = jnp.take(group, order, axis=0)
+    return group.reshape((ncols * piece.shape[0],) + piece.shape[1:])
+
+
 def body(vectors, tile_vals, tile_row, tile_src, send_list, ritz_matrix):
-    first_pass = apply_operator(vectors, tile_vals, tile_row, tile_src, send_list).astype(
+    tile_side = tile_vals.shape[1]
+    nblocks = vectors.shape[1] // tile_side
+    nrows = lax.axis_size("rows")
+    ncols = lax.axis_size("cols")
+    slot = send_list.shape[1]
+    src_ids = remap_sources(tile_src, nblocks, slot, nrows)
+    first_pass = apply_operator(vectors, tile_vals, tile_row, src_ids, send_list).astype(
         jnp.bfloat16
     )
-    second = apply_operator(first_pass, tile_vals, tile_row, tile_src, send_list)
+    second = apply_operator(first_pass, tile_vals, tile_row, src_ids, send_list)
     filtered = (2.0 * second - vectors.astype(jnp.float32)).astype(jnp.bfloat16)
-    total_nodes = vectors.shape[1] * lax.axis_size("rows")
-    operated = apply_operator(filtered, tile_vals, tile_row, tile_src, send_list).astype(
+    total_nodes = vectors.shape[1] * nrows
+    portion = gather_cols(filtered, ncols)
+    operated = apply_operator(filtered, tile_vals, tile_row, src_ids, send_list).astype(
         jnp.bfloat16
     )
-    portion = lax.all_gather(filtered, "cols", axis=0, tiled=True)
     gram_piece = contract_nodes(filtered, portion)
     proj_piece = contract_nodes(operated, portion)
     turned = lax.dot_general(
         ritz_matrix, portion, (((0,), (0,)), ((), ())), preferred_element_type=jnp.float32
     )
-    gram_total, proj_total = lax.psum((gram_piece, proj_piece), "rows")
-    gram_matrix = gram_total / total_nodes
-    projected = proj_total / total_nodes
+    both = tree_sum_rows(jnp.stack([gram_piece, proj_piece]), nrows)
+    gram_matrix = both[0] / total_nodes
+    projected = both[1] / total_nodes
     rotated = turned.astype(jnp.bfloat16)
     return (rotated, gram_matrix, projected)
 

time: 208 us -> 191 us (0.918)
  blocking collectives: 64.2 us -> 0 us
  starting transfers between devices: 11.9 us -> 61.5 us
  waiting for transfers between devices: 50.6 us -> 26.6 us
  local copies, waits for them, and re-layouts: 11.7 us -> 31.9 us
  other arithmetic: 4.96 us -> 19.8 us
  between operations: 14.2 us -> 1.79 us
    ppermute x0 -> x26, starting transfers between devices: none -> 61.5 us  [the longest x21 57.1 us: apply_operator(): chunk = lax.ppermute(chunk, 'rows', pairs)]
    all_to_all x2 -> x0, waiting for transfers between devices: 50.1 us -> none  [apply_operator(): lax.all_to_all(outgoing, 'rows', split_axis=1, concat_axis=1, tiled=True)]
    psum x1 -> x0, blocking collectives: 35 us -> none  [body(): gram_total, proj_total = lax.psum((gram_piece, proj_piece), 'rows')]
    all_to_all x1 -> x0, blocking collectives: 29.3 us -> none  [apply_operator(): lax.all_to_all(outgoing, 'rows', split_axis=1, concat_axis=1, tiled=True)]
    ppermute x0 -> x26, waiting for transfers between devices: none -> 26.6 us  [the longest x21 18.5 us: apply_operator(): chunk = lax.ppermute(chunk, 'rows', pairs)]
    gather x3 -> x25, local copies, waits for them, and re-layouts: 1.94 us -> 17.9 us  [the longest x24 15.5 us: apply_operator(): chunk = jnp.take(blocked, wanted, axis=1)]
    all_to_all x2 -> x0, starting transfers between devices: 11.6 us -> none  [apply_operator(): lax.all_to_all(outgoing, 'rows', split_axis=1, concat_axis=1, tiled=True)]
    select_n x5 -> x26, other arithmetic: 2.6 us -> 8.89 us  [the longest x21 4.43 us: apply_operator(): chunk = jnp.take(blocked, wanted, axis=1)]
  transfers between devices with their start and end apart: 3 -> 26, of which waited for: 2 -> 8; matrix products, arithmetic and copies ran while one was open for 9% -> 19% of each run, Pallas kernels for 0% -> 0%
where the time goes in v1:
time: 191 us; the launch traced here: 190 us
  starting transfers between devices  61.5 us (32%)
  matrix products  48.9 us (26%)
  local copies, waits for them, and re-layouts  31.9 us (17%)
  waiting for transfers between devices  26.6 us (14%)
  other arithmetic  19.8 us (10%)
    ppermute x21, starting transfers between devices, apply_operator(): chunk = lax.ppermute(chunk, 'rows', pairs)  57.1 us
    dot_general x3, matrix products, tile_products(): jnp.einsum('ktc,trc->ktr', chosen, tile_block, preferred_element_type=jnp...  36.1 us
    ppermute x21, waiting for transfers between devices, apply_operator(): chunk = lax.ppermute(chunk, 'rows', pairs)  18.5 us
    gather x24, local copies, waits for them, and re-layouts, apply_operator(): chunk = jnp.take(blocked, wanted, axis=1)  15.5 us
    dot_general x3, matrix products, tile_products(): jnp.einsum('bt,ktr->kbr', onehot, products, precision=lax.Precision.HIGHEST)  10.3 us
    ppermute x3, waiting for transfers between devices, tree_sum_rows(): value = value + lax.ppermute(value, 'rows', pairs)  8.11 us
    gather x3, local copies, waits for them, and re-layouts, tile_products(): chosen = jnp.take(sources, src_ids, axis=1)  6.12 us
    select_n x21, other arithmetic, apply_operator(): chunk = jnp.take(blocked, wanted, axis=1)  4.43 us
  transfers between devices with their start and end apart: 26, of which 8 were waited for; matrix products, arithmetic and copies ran while one was open for 19% of the time, Pallas kernels for 0%

profile of v1, /device:TPU:0, one launch (start us, length us, event | category | flops | bytes accessed | tf_op | source)
XLA Modules:
  0.0 190.5 jit_solution(2919103307769515074)
XLA Ops:
  4.2 6.1 %collective-permute-start.6 = (bf16[16,16,256]{2,0,1:T(8,128)(2,1)S(1)}, bf16[16,16,256]{2,0,1:T(8,128)(2,1)S(1)}, u32[]{:S(2)}, u32[]{:S(2)}) collective-permute-start(bf16[16,16,256]{2,0,1:T(8,128)(2,1)S(1)} %select_bitcast_fusion.7), channel_id=1, source_target_pairs={{0,28},{4,0},{8,4},{12,8},{16,12},{20,16},{24,20},{28,24},{1,29},{... | collective-permute-start | bytes 393224 | tf_op jit(solution)/shard_map/ppermute | solution.py:38
  13.1 2.5 %collective-permute-start.2 = (bf16[16,16,256]{2,0,1:T(8,128)(2,1)S(1)}, bf16[16,16,256]{2,0,1:T(8,128)(2,1)S(1)}, u32[]{:S(2)}, u32[]{:S(2)}) collective-permute-start(bf16[16,16,256]{2,0,1:T(8,128)(2,1)S(1)} %select_bitcast_fusion.11), channel_id=1, source_target_pairs={{0,12},{4,16},{8,20},{12,24},{16,28},{20,0},{24,4},{28,8},{1,13},{... | collective-permute-start | bytes 393224 | tf_op jit(solution)/shard_map/ppermute | solution.py:38
  16.9 2.8 %collective-permute-start.3 = (bf16[16,16,256]{2,0,1:T(8,128)(2,1)}, bf16[16,16,256]{2,0,1:T(8,128)(2,1)}, u32[]{:S(2)}, u32[]{:S(2)}) collective-permute-start(bf16[16,16,256]{2,0,1:T(8,128)(2,1)} %select_bitcast_fusion.10), channel_id=1, source_target_pairs={{0,16},{4,20},{8,24},{12,28},{16,0},{20,4},{24,8},{28,12},{1,17},{... | collective-permute-start | bytes 393224 | tf_op jit(solution)/shard_map/ppermute | solution.py:38
  31.6 2.8 %collective-permute-start.5 = (bf16[16,16,256]{2,0,1:T(8,128)(2,1)S(1)}, bf16[16,16,256]{2,0,1:T(8,128)(2,1)S(1)}, u32[]{:S(2)}, u32[]{:S(2)}) collective-permute-start(bf16[16,16,256]{2,0,1:T(8,128)(2,1)S(1)} %select_bitcast_fusion.8), channel_id=1, source_target_pairs={{0,24},{4,28},{8,0},{12,4},{16,8},{20,12},{24,16},{28,20},{1,25},{... | collective-permute-start | bytes 393224 | tf_op jit(solution)/shard_map/ppermute | solution.py:38
  35.3 3.2 %collective-permute-done.4 = bf16[16,16,256]{2,0,1:T(8,128)(2,1)S(1)} collective-permute-done((bf16[16,16,256]{2,0,1:T(8,128)(2,1)S(1)}, bf16[16,16,256]{2,0,1:T(8,128)(2,1)S(1)}, u32[]{:S(2)}, u32[]{:S(2)}) %collective-permute-start.4) | collective-permute-done | bytes 131104 | tf_op jit(solution)/shard_map/ppermute | solution.py:38
  40.6 12.0 %convolution_bitcast_fusion.2 = f32[16,192,256]{2,0,1:T(8,128)S(1)} fusion(bf16[192,256,256]{2,1,0:T(8,128)(2,1)} %param.11, bf16[192,16,256]{2,1,0:T(8,128)(2,1)} %gather_fusion.9, pred[192]{0:T(512)(128)(4,1)S(1)} %get-tuple-element.5), kind=kOutput, calls=%fused_computation.42 | convolution fusion | flops 403439616 | bytes 29884608 | tf_op jit(solution)/shard_map/ktc,trc->ktr/dot_general | solution.py:9
  52.7 4.0 %constant_dynamic-update-slice_fusion.15 = (bf16[16,192,256]{2,1,0:T(8,128)(2,1)}, bf16[16,64,256]{2,1,0:T(8,128)(2,1)S(1)}) fusion(s32[192]{0:T(256)S(1)} %bitcast.190, f32[16,192,256]{2,0,1:T(8,128)S(1)} %convolution_bitcast_fusion.2), kind=kOutput, calls=%fused_computation.114 | convolution fusion | flops 604254208 | bytes 4195072 | tf_op jit(solution)/shard_map/bt,ktr->kbr/dot_general | solution.py:11
  63.3 3.1 %collective-permute-start.7 = (bf16[16,16,256]{2,1,0:T(8,128)(2,1)S(1)}, bf16[16,16,256]{2,1,0:T(8,128)(2,1)S(1)}, u32[]{:S(2)}, u32[]{:S(2)}) collective-permute-start(bf16[16,16,256]{2,1,0:T(8,128)(2,1)S(1)} %fusion.37), channel_id=1, source_target_pairs={{0,4},{4,8},{8,12},{12,16},{16,20},{20,24},{24,28},{28,0},{1,5},{5... | collective-permute-start | bytes 393224 | tf_op jit(solution)/shard_map/ppermute | solution.py:38
  69.1 3.6 %collective-permute-start.10 = (bf16[16,16,256]{2,1,0:T(8,128)(2,1)S(1)}, bf16[16,16,256]{2,1,0:T(8,128)(2,1)S(1)}, u32[]{:S(2)}, u32[]{:S(2)}) collective-permute-start(bf16[16,16,256]{2,1,0:T(8,128)(2,1)S(1)} %fusion.34), channel_id=1, source_target_pairs={{0,16},{4,20},{8,24},{12,28},{16,0},{20,4},{24,8},{28,12},{1,17},{... | collective-permute-start | bytes 393224 | tf_op jit(solution)/shard_map/ppermute | solution.py:38
  77.0 6.4 %collective-permute-done.9 = bf16[16,16,256]{2,1,0:T(8,128)(2,1)S(1)} collective-permute-done((bf16[16,16,256]{2,1,0:T(8,128)(2,1)S(1)}, bf16[16,16,256]{2,1,0:T(8,128)(2,1)S(1)}, u32[]{:S(2)}, u32[]{:S(2)}) %collective-permute-start.9) | collective-permute-done | bytes 131104 | tf_op jit(solution)/shard_map/ppermute | solution.py:38
  87.5 12.0 %convolution_bitcast_fusion.1 = f32[16,192,256]{2,0,1:T(8,128)S(1)} fusion(bf16[192,256,256]{2,1,0:T(8,128)(2,1)} %param.11, bf16[192,16,256]{2,1,0:T(8,128)(2,1)} %gather_fusion.18, pred[192]{0:T(512)(128)(4,1)S(1)} %get-tuple-element.5), kind=kOutput, calls=%fused_computation.41 | convolution fusion | flops 403439616 | bytes 29884608 | tf_op jit(solution)/shard_map/ktc,trc->ktr/dot_general | solution.py:9
  99.5 3.2 %fusion.16 = f32[16,256,64]{1,2,0:T(8,128)S(1)} fusion(f32[16,192,256]{2,0,1:T(8,128)S(1)} %convolution_bitcast_fusion.1, s32[192]{0:T(256)S(1)} %bitcast.191), kind=kOutput, calls=%fused_computation.52 | convolution fusion | flops 604254208 | bytes 4195072 | tf_op jit(solution)/shard_map/bt,ktr->kbr/dot_general | solution.py:11
  111.7 8.9 %collective-permute-start.22 = (bf16[16,16,256]{2,0,1:T(8,128)(2,1)S(1)}, bf16[16,16,256]{2,0,1:T(8,128)(2,1)S(1)}, u32[]{:S(2)}, u32[]{:S(2)}) collective-permute-start(bf16[16,16,256]{2,0,1:T(8,128)(2,1)S(1)} %select_bitcast_fusion), channel_id=1, source_target_pairs={{0,28},{4,0},{8,4},{12,8},{16,12},{20,16},{24,20},{28,24},{1,29},{... | collective-permute-start | bytes 393224 | tf_op jit(solution)/shard_map/ppermute | solution.py:38
  124.4 5.4 %collective-permute-done.16 = bf16[16,16,256]{2,0,1:T(8,128)(2,1)S(1)} collective-permute-done((bf16[16,16,256]{2,0,1:T(8,128)(2,1)S(1)}, bf16[16,16,256]{2,0,1:T(8,128)(2,1)S(1)}, u32[]{:S(2)}, u32[]{:S(2)}) %collective-permute-start.16) | collective-permute-done | bytes 131104 | tf_op jit(solution)/shard_map/ppermute | solution.py:38
  129.8 10.2 %collective-permute-start.19 = (bf16[16,16,256]{2,0,1:T(8,128)(2,1)S(1)}, bf16[16,16,256]{2,0,1:T(8,128)(2,1)S(1)}, u32[]{:S(2)}, u32[]{:S(2)}) collective-permute-start(bf16[16,16,256]{2,0,1:T(8,128)(2,1)S(1)} %select_bitcast_fusion.3), channel_id=1, source_target_pairs={{0,16},{4,20},{8,24},{12,28},{16,0},{20,4},{24,8},{28,12},{1,17},{... | collective-permute-start | bytes 393224 | tf_op jit(solution)/shard_map/ppermute | solution.py:38
  140.0 2.8 %collective-permute-start.20 = (bf16[16,16,256]{2,0,1:T(8,128)(2,1)S(1)}, bf16[16,16,256]{2,0,1:T(8,128)(2,1)S(1)}, u32[]{:S(2)}, u32[]{:S(2)}) collective-permute-start(bf16[16,16,256]{2,0,1:T(8,128)(2,1)S(1)} %select_bitcast_fusion.2), channel_id=1, source_target_pairs={{0,20},{4,24},{8,28},{12,0},{16,4},{20,8},{24,12},{28,16},{1,21},{... | collective-permute-start | bytes 393224 | tf_op jit(solution)/shard_map/ppermute | solution.py:38
  142.8 3.6 %collective-permute-start.21 = (bf16[16,16,256]{2,0,1:T(8,128)(2,1)S(1)}, bf16[16,16,256]{2,0,1:T(8,128)(2,1)S(1)}, u32[]{:S(2)}, u32[]{:S(2)}) collective-permute-start(bf16[16,16,256]{2,0,1:T(8,128)(2,1)S(1)} %select_bitcast_fusion.1), channel_id=1, source_target_pairs={{0,24},{4,28},{8,0},{12,4},{16,8},{20,12},{24,16},{28,20},{1,25},{... | collective-permute-start | bytes 393224 | tf_op jit(solution)/shard_map/ppermute | solution.py:38
  151.0 2.5 %fusion.70 = (bf16[2,1,16,16384]{3,2,1,0:T(8,128)(2,1)}, bf16[2,16,16384]{2,1,0:T(8,128)(2,1)}) fusion(bf16[1,16,16384]{2,1,0:T(8,128)(2,1)} %bitcast.35, bf16[1,16,16384]{2,1,0:T(8,128)(2,1)S(1)} %bitcast.165), kind=kLoop, calls=%fused_computation.211 | loop fusion | flops 524288 | bytes 3145728 | tf_op jit(solution)/shard_map/stack | solution.py:73
  153.5 12.0 %convolution_bitcast_fusion = f32[16,192,256]{2,0,1:T(8,128)S(1)} fusion(bf16[192,256,256]{2,1,0:T(8,128)(2,1)} %param.11, bf16[192,16,256]{2,1,0:T(8,128)(2,1)} %gather_fusion.27, pred[192]{0:T(512)(128)(4,1)S(1)} %get-tuple-element.5), kind=kOutput, calls=%fused_computation.40 | convolution fusion | flops 403439616 | bytes 29884608 | tf_op jit(solution)/shard_map/ktc,trc->ktr/dot_general | solution.py:9
  165.5 3.2 %fusion.22 = bf16[16,256,64]{1,2,0:T(8,128)(2,1)S(1)} fusion(f32[16,192,256]{2,0,1:T(8,128)S(1)} %convolution_bitcast_fusion, s32[192]{0:T(256)S(1)} %bitcast.192), kind=kOutput, calls=%fused_computation.54 | convolution fusion | flops 604254208 | bytes 3670784 | tf_op jit(solution)/shard_map/bt,ktr->kbr/dot_general | solution.py:11
  169.0 3.3 %maximum_select_fusion = bf16[2,2,16,16384]{3,2,1,0:T(8,128)(2,1)} fusion(bf16[2,1,16,16384]{3,2,1,0:T(8,128)(2,1)} %bitcast.37, bf16[2,1,16,16384]{3,2,1,0:T(8,128)(2,1)S(1)} %copy-done.5, pred[]{:T(512)S(6)} %eq.64), kind=kLoop, calls=%fused_computation.37 | loop fusion | flops 3145728 | bytes 4194305 | tf_op jit(solution)/shard_map/jit(_where)/select_n | solution.py:73
  177.7 3.7 %collective-permute-done.23 = f32[2,16,64]{2,1,0:T(8,128)S(1)} collective-permute-done((f32[2,16,64]{2,1,0:T(8,128)S(1)}, f32[2,16,64]{2,1,0:T(8,128)S(1)}, u32[]{:S(2)}, u32[]{:S(2)}) %collective-permute-start.23) | collective-permute-done | bytes 8224 | tf_op jit(solution)/shard_map/ppermute | solution.py:55
  181.5 3.7 %collective-permute-done.24 = f32[2,16,64]{2,1,0:T(8,128)S(1)} collective-permute-done((f32[2,16,64]{2,1,0:T(8,128)S(1)}, f32[2,16,64]{2,1,0:T(8,128)S(1)}, u32[]{:S(2)}, u32[]{:S(2)}) %collective-permute-start.24) | collective-permute-done | bytes 8224 | tf_op jit(solution)/shard_map/ppermute | solution.py:55
  185.2 2.8 %collective-permute-start.25 = (f32[2,16,64]{2,1,0:T(8,128)S(1)}, f32[2,16,64]{2,1,0:T(8,128)S(1)}, u32[]{:S(2)}, u32[]{:S(2)}) collective-permute-start(f32[2,16,64]{2,1,0:T(8,128)S(1)} %fusion.80), channel_id=1, source_target_pairs={{0,16},{4,20},{8,24},{12,28},{16,0},{20,4},{24,8},{28,12},{1,17},{... | collective-permute-start | bytes 24584 | tf_op jit(solution)/shard_map/ppermute | solution.py:55
  (207 shorter events, 65.0 us)
Async XLA Ops:
  4.2 34.3 %collective-permute-start.6 = (bf16[16,16,256]{2,0,1:T(8,128)(2,1)S(1)}, bf16[16,16,256]{2,0,1:T(8,128)(2,1)S(1)}, u32[]{:S(2)}, u32[]{:S(2)}) collective-permute-start(bf16[16,16,256]{2,0,1:T(8,128)(2,1)S(1)} %select_bitcast_fusion.7), channel_id=1, source_target_pairs={{0,28},{4,0},{8,4},{12,8},{16,12},{20,16},{24,20},{28,24},{1,29},{... | collective-permute-start | bytes 393224 | tf_op jit(solution)/shard_map/ppermute | solution.py:38
  11.6 19.8 %collective-permute-start = (bf16[16,16,256]{2,0,1:T(8,128)(2,1)}, bf16[16,16,256]{2,0,1:T(8,128)(2,1)S(1)}, u32[]{:S(2)}, u32[]{:S(2)}) collective-permute-start(bf16[16,16,256]{2,0,1:T(8,128)(2,1)} %select_bitcast_fusion.13), channel_id=1, source_target_pairs={{0,4},{4,8},{8,12},{12,16},{16,20},{20,24},{24,28},{28,0},{1,5},{5... | collective-permute-start | bytes 393224 | tf_op jit(solution)/shard_map/ppermute | solution.py:38
  12.3 19.3 %collective-permute-start.1 = (bf16[16,16,256]{2,0,1:T(8,128)(2,1)S(1)}, bf16[16,16,256]{2,0,1:T(8,128)(2,1)S(1)}, u32[]{:S(2)}, u32[]{:S(2)}) collective-permute-start(bf16[16,16,256]{2,0,1:T(8,128)(2,1)S(1)} %select_bitcast_fusion.12), channel_id=1, source_target_pairs={{0,8},{4,12},{8,16},{12,20},{16,24},{20,28},{24,0},{28,4},{1,9},{5... | collective-permute-start | bytes 393224 | tf_op jit(solution)/shard_map/ppermute | solution.py:38
  13.1 21.3 %collective-permute-start.2 = (bf16[16,16,256]{2,0,1:T(8,128)(2,1)S(1)}, bf16[16,16,256]{2,0,1:T(8,128)(2,1)S(1)}, u32[]{:S(2)}, u32[]{:S(2)}) collective-permute-start(bf16[16,16,256]{2,0,1:T(8,128)(2,1)S(1)} %select_bitcast_fusion.11), channel_id=1, source_target_pairs={{0,12},{4,16},{8,20},{12,24},{16,28},{20,0},{24,4},{28,8},{1,13},{... | collective-permute-start | bytes 393224 | tf_op jit(solution)/shard_map/ppermute | solution.py:38
  16.9 17.5 %collective-permute-start.3 = (bf16[16,16,256]{2,0,1:T(8,128)(2,1)}, bf16[16,16,256]{2,0,1:T(8,128)(2,1)}, u32[]{:S(2)}, u32[]{:S(2)}) collective-permute-start(bf16[16,16,256]{2,0,1:T(8,128)(2,1)} %select_bitcast_fusion.10), channel_id=1, source_target_pairs={{0,16},{4,20},{8,24},{12,28},{16,0},{20,4},{24,8},{28,12},{1,17},{... | collective-permute-start | bytes 393224 | tf_op jit(solution)/shard_map/ppermute | solution.py:38
  31.4 7.1 %collective-permute-start.4 = (bf16[16,16,256]{2,0,1:T(8,128)(2,1)S(1)}, bf16[16,16,256]{2,0,1:T(8,128)(2,1)S(1)}, u32[]{:S(2)}, u32[]{:S(2)}) collective-permute-start(bf16[16,16,256]{2,0,1:T(8,128)(2,1)S(1)} %select_bitcast_fusion.9), channel_id=1, source_target_pairs={{0,20},{4,24},{8,28},{12,0},{16,4},{20,8},{24,12},{28,16},{1,21},{... | collective-permute-start | bytes 393224 | tf_op jit(solution)/shard_map/ppermute | solution.py:38
  31.6 6.9 %collective-permute-start.5 = (bf16[16,16,256]{2,0,1:T(8,128)(2,1)S(1)}, bf16[16,16,256]{2,0,1:T(8,128)(2,1)S(1)}, u32[]{:S(2)}, u32[]{:S(2)}) collective-permute-start(bf16[16,16,256]{2,0,1:T(8,128)(2,1)S(1)} %select_bitcast_fusion.8), channel_id=1, source_target_pairs={{0,24},{4,28},{8,0},{12,4},{16,8},{20,12},{24,16},{28,20},{1,25},{... | collective-permute-start | bytes 393224 | tf_op jit(solution)/shard_map/ppermute | solution.py:38
  63.3 10.7 %collective-permute-start.7 = (bf16[16,16,256]{2,1,0:T(8,128)(2,1)S(1)}, bf16[16,16,256]{2,1,0:T(8,128)(2,1)S(1)}, u32[]{:S(2)}, u32[]{:S(2)}) collective-permute-start(bf16[16,16,256]{2,1,0:T(8,128)(2,1)S(1)} %fusion.37), channel_id=1, source_target_pairs={{0,4},{4,8},{8,12},{12,16},{16,20},{20,24},{24,28},{28,0},{1,5},{5... | collective-permute-start | bytes 393224 | tf_op jit(solution)/shard_map/ppermute | solution.py:38
  66.4 8.8 %collective-permute-start.8 = (bf16[16,16,256]{2,1,0:T(8,128)(2,1)S(1)}, bf16[16,16,256]{2,1,0:T(8,128)(2,1)S(1)}, u32[]{:S(2)}, u32[]{:S(2)}) collective-permute-start(bf16[16,16,256]{2,1,0:T(8,128)(2,1)S(1)} %fusion.36), channel_id=1, source_target_pairs={{0,8},{4,12},{8,16},{12,20},{16,24},{20,28},{24,0},{28,4},{1,9},{5... | collective-permute-start | bytes 393224 | tf_op jit(solution)/shard_map/ppermute | solution.py:38
  67.5 15.9 %collective-permute-start.9 = (bf16[16,16,256]{2,1,0:T(8,128)(2,1)S(1)}, bf16[16,16,256]{2,1,0:T(8,128)(2,1)S(1)}, u32[]{:S(2)}, u32[]{:S(2)}) collective-permute-start(bf16[16,16,256]{2,1,0:T(8,128)(2,1)S(1)} %fusion.35), channel_id=1, source_target_pairs={{0,12},{4,16},{8,20},{12,24},{16,28},{20,0},{24,4},{28,8},{1,13},{... | collective-permute-start | bytes 393224 | tf_op jit(solution)/shard_map/ppermute | solution.py:38
  69.1 15.3 %collective-permute-start.10 = (bf16[16,16,256]{2,1,0:T(8,128)(2,1)S(1)}, bf16[16,16,256]{2,1,0:T(8,128)(2,1)S(1)}, u32[]{:S(2)}, u32[]{:S(2)}) collective-permute-start(bf16[16,16,256]{2,1,0:T(8,128)(2,1)S(1)} %fusion.34), channel_id=1, source_target_pairs={{0,16},{4,20},{8,24},{12,28},{16,0},{20,4},{24,8},{28,12},{1,17},{... | collective-permute-start | bytes 393224 | tf_op jit(solution)/shard_map/ppermute | solution.py:38
  72.7 11.8 %collective-permute-start.11 = (bf16[16,16,256]{2,1,0:T(8,128)(2,1)S(1)}, bf16[16,16,256]{2,1,0:T(8,128)(2,1)S(1)}, u32[]{:S(2)}, u32[]{:S(2)}) collective-permute-start(bf16[16,16,256]{2,1,0:T(8,128)(2,1)S(1)} %fusion.33), channel_id=1, source_target_pairs={{0,20},{4,24},{8,28},{12,0},{16,4},{20,8},{24,12},{28,16},{1,21},{... | collective-permute-start | bytes 393224 | tf_op jit(solution)/shard_map/ppermute | solution.py:38
  74.1 10.4 %collective-permute-start.12 = (bf16[16,16,256]{2,1,0:T(8,128)(2,1)S(1)}, bf16[16,16,256]{2,1,0:T(8,128)(2,1)S(1)}, u32[]{:S(2)}, u32[]{:S(2)}) collective-permute-start(bf16[16,16,256]{2,1,0:T(8,128)(2,1)S(1)} %fusion.32), channel_id=1, source_target_pairs={{0,24},{4,28},{8,0},{12,4},{16,8},{20,12},{24,16},{28,20},{1,25},{... | collective-permute-start | bytes 393224 | tf_op jit(solution)/shard_map/ppermute | solution.py:38
  75.3 9.3 %collective-permute-start.13 = (bf16[16,16,256]{2,1,0:T(8,128)(2,1)S(1)}, bf16[16,16,256]{2,1,0:T(8,128)(2,1)S(1)}, u32[]{:S(2)}, u32[]{:S(2)}) collective-permute-start(bf16[16,16,256]{2,1,0:T(8,128)(2,1)S(1)} %fusion.31), channel_id=1, source_target_pairs={{0,28},{4,0},{8,4},{12,8},{16,12},{20,16},{24,20},{28,24},{1,29},{... | collective-permute-start | bytes 393224 | tf_op jit(solution)/shard_map/ppermute | solution.py:38
  109.4 41.6 %collective-permute-start.14 = (bf16[16,16384]{1,0:T(8,128)(2,1)S(1)}, bf16[16,16384]{1,0:T(8,128)(2,1)}, u32[]{:S(2)}, u32[]{:S(2)}) collective-permute-start(bf16[16,16384]{1,0:T(8,128)(2,1)S(1)} %subtract_convert_fusion), channel_id=1, source_target_pairs={{0,2},{1,3},{2,0},{3,1},{4,6},{5,7},{6,4},{7,5},{8,10},{9,11},{10,... | collective-permute-start | bytes 1572872 | tf_op jit(solution)/shard_map/ppermute | solution.py:66
  111.7 37.2 %collective-permute-start.22 = (bf16[16,16,256]{2,0,1:T(8,128)(2,1)S(1)}, bf16[16,16,256]{2,0,1:T(8,128)(2,1)S(1)}, u32[]{:S(2)}, u32[]{:S(2)}) collective-permute-start(bf16[16,16,256]{2,0,1:T(8,128)(2,1)S(1)} %select_bitcast_fusion), channel_id=1, source_target_pairs={{0,28},{4,0},{8,4},{12,8},{16,12},{20,16},{24,20},{28,24},{1,29},{... | collective-permute-start | bytes 393224 | tf_op jit(solution)/shard_map/ppermute | solution.py:38
  120.6 9.2 %collective-permute-start.16 = (bf16[16,16,256]{2,0,1:T(8,128)(2,1)S(1)}, bf16[16,16,256]{2,0,1:T(8,128)(2,1)S(1)}, u32[]{:S(2)}, u32[]{:S(2)}) collective-permute-start(bf16[16,16,256]{2,0,1:T(8,128)(2,1)S(1)} %select_bitcast_fusion.6), channel_id=1, source_target_pairs={{0,4},{4,8},{8,12},{12,16},{16,20},{20,24},{24,28},{28,0},{1,5},{5... | collective-permute-start | bytes 393224 | tf_op jit(solution)/shard_map/ppermute | solution.py:38
  120.6 19.4 %collective-permute-start.17 = (bf16[16,16,256]{2,0,1:T(8,128)(2,1)S(1)}, bf16[16,16,256]{2,0,1:T(8,128)(2,1)S(1)}, u32[]{:S(2)}, u32[]{:S(2)}) collective-permute-start(bf16[16,16,256]{2,0,1:T(8,128)(2,1)S(1)} %select_bitcast_fusion.5), channel_id=1, source_target_pairs={{0,8},{4,12},{8,16},{12,20},{16,24},{20,28},{24,0},{28,4},{1,9},{5... | collective-permute-start | bytes 393224 | tf_op jit(solution)/shard_map/ppermute | solution.py:38
  122.0 20.8 %collective-permute-start.18 = (bf16[16,16,256]{2,0,1:T(8,128)(2,1)S(1)}, bf16[16,16,256]{2,0,1:T(8,128)(2,1)S(1)}, u32[]{:S(2)}, u32[]{:S(2)}) collective-permute-start(bf16[16,16,256]{2,0,1:T(8,128)(2,1)S(1)} %select_bitcast_fusion.4), channel_id=1, source_target_pairs={{0,12},{4,16},{8,20},{12,24},{16,28},{20,0},{24,4},{28,8},{1,13},{... | collective-permute-start | bytes 393224 | tf_op jit(solution)/shard_map/ppermute | solution.py:38
  129.8 16.6 %collective-permute-start.19 = (bf16[16,16,256]{2,0,1:T(8,128)(2,1)S(1)}, bf16[16,16,256]{2,0,1:T(8,128)(2,1)S(1)}, u32[]{:S(2)}, u32[]{:S(2)}) collective-permute-start(bf16[16,16,256]{2,0,1:T(8,128)(2,1)S(1)} %select_bitcast_fusion.3), channel_id=1, source_target_pairs={{0,16},{4,20},{8,24},{12,28},{16,0},{20,4},{24,8},{28,12},{1,17},{... | collective-permute-start | bytes 393224 | tf_op jit(solution)/shard_map/ppermute | solution.py:38
  140.0 6.4 %collective-permute-start.20 = (bf16[16,16,256]{2,0,1:T(8,128)(2,1)S(1)}, bf16[16,16,256]{2,0,1:T(8,128)(2,1)S(1)}, u32[]{:S(2)}, u32[]{:S(2)}) collective-permute-start(bf16[16,16,256]{2,0,1:T(8,128)(2,1)S(1)} %select_bitcast_fusion.2), channel_id=1, source_target_pairs={{0,20},{4,24},{8,28},{12,0},{16,4},{20,8},{24,12},{28,16},{1,21},{... | collective-permute-start | bytes 393224 | tf_op jit(solution)/shard_map/ppermute | solution.py:38
  142.8 6.1 %collective-permute-start.21 = (bf16[16,16,256]{2,0,1:T(8,128)(2,1)S(1)}, bf16[16,16,256]{2,0,1:T(8,128)(2,1)S(1)}, u32[]{:S(2)}, u32[]{:S(2)}) collective-permute-start(bf16[16,16,256]{2,0,1:T(8,128)(2,1)S(1)} %select_bitcast_fusion.1), channel_id=1, source_target_pairs={{0,24},{4,28},{8,0},{12,4},{16,8},{20,12},{24,16},{28,20},{1,25},{... | collective-permute-start | bytes 393224 | tf_op jit(solution)/shard_map/ppermute | solution.py:38
  153.5 15.5 %collective-permute-start.15 = (bf16[2,16,16384]{2,1,0:T(8,128)(2,1)}, bf16[2,16,16384]{2,1,0:T(8,128)(2,1)}, u32[]{:S(2)}, u32[]{:S(2)}) collective-permute-start(bf16[2,16,16384]{2,1,0:T(8,128)(2,1)} %get-tuple-element.24), channel_id=1, source_target_pairs={{0,1},{1,0},{2,3},{3,2},{4,5},{5,4},{6,7},{7,6},{8,9},{9,8},{10,11... | collective-permute-start | bytes 3145736 | tf_op jit(solution)/shard_map/ppermute | solution.py:70
  185.2 4.6 %collective-permute-start.25 = (f32[2,16,64]{2,1,0:T(8,128)S(1)}, f32[2,16,64]{2,1,0:T(8,128)S(1)}, u32[]{:S(2)}, u32[]{:S(2)}) collective-permute-start(f32[2,16,64]{2,1,0:T(8,128)S(1)} %fusion.80), channel_id=1, source_target_pairs={{0,16},{4,20},{8,24},{12,28},{16,0},{20,4},{24,8},{28,12},{1,17},{... | collective-permute-start | bytes 24584 | tf_op jit(solution)/shard_map/ppermute | solution.py:55
  (32 other events, 400.7 us)

commit v2 on v1

v2 whole, which is shorter than its diff:
```python
import functools

import jax
import jax.numpy as jnp
from jax import lax
from jax.experimental import pallas as pl
from jax.experimental.pallas import tpu as pltpu
from jax.sharding import PartitionSpec as P

NBUF = 8


def tile_kernel(order_ref, row_ref, src_ref, *refs, first, counts):
    nsrc = len(counts)
    sources = refs[:nsrc]
    tiles_hbm = refs[nsrc]
    out_ref = refs[nsrc + 1]
    buf = refs[nsrc + 2]
    sem = refs[nsrc + 3]
    total = sum(counts)
    out_ref[...] = jnp.zeros(out_ref.shape, out_ref.dtype)

    def copy(j, slot):
        return pltpu.make_async_copy(tiles_hbm.at[order_ref[first + j]], buf.at[slot], sem.at[slot])

    for j in range(min(NBUF, total)):
        copy(j, j).start()
    base = 0
    for k, cnt in enumerate(counts):

        def step(q, carry, k=k, base=base):
            j = base + q
            slot = j % NBUF
            copy(j, slot).wait()
            lhs = sources[k][src_ref[first + j]]
            prod = lax.dot_general(
                lhs, buf[slot], (((1,), (1,)), ((), ())), preferred_element_type=jnp.float32
            )
            r = row_ref[first + j]
            out_ref[r] = out_ref[r] + prod

            @pl.when(j + NBUF < total)
            def _():
                copy(j + NBUF, slot).start()

            return carry

        lax.fori_loop(0, cnt, step, 0)
        base += cnt


def run_tiles(order, rowof, srcof, sources, tile_vals, first, counts, nblocks):
    columns, side = sources[0].shape[1], sources[0].shape[2]
    kernel = functools.partial(tile_kernel, first=first, counts=tuple(counts))
    in_specs = [pl.BlockSpec(memory_space=pltpu.VMEM) for _ in sources]
    in_specs.append(pl.BlockSpec(memory_space=pl.ANY))
    return pl.pallas_call(
        kernel,
        out_shape=jax.ShapeDtypeStruct((nblocks, columns, side), jnp.float32),
        grid_spec=pltpu.PrefetchScalarGridSpec(
            num_scalar_prefetch=3,
            grid=(1,),
            in_specs=in_specs,
            out_specs=pl.BlockSpec(memory_space=pltpu.VMEM),
            scratch_shapes=[
                pltpu.VMEM((NBUF,) + tile_vals.shape[1:], tile_vals.dtype),
                pltpu.SemaphoreType.DMA((NBUF,)),
            ],
        ),
    )(order, rowof, srcof, *sources, tile_vals)


def plan_slots(tile_row, tile_src, send_list):
    nrows, slot = send_list.shape
    ntiles = tile_src.shape[-1]
    nblocks = ntiles - nrows * slot
    me = lax.axis_index("rows")
    src = tile_src.reshape(-1)
    peer = (src - nblocks) // slot
    shift = (me - peer) % nrows
    moved = nblocks + shift * slot + (src - nblocks) % slot
    slots = jnp.where(src < nblocks, src, moved)
    order = jnp.zeros((ntiles,), jnp.int32).at[slots].set(jnp.arange(ntiles, dtype=jnp.int32))
    rowof = jnp.take(tile_row.reshape(-1), order)
    j = jnp.arange(ntiles, dtype=jnp.int32)
    mine = lax.dynamic_index_in_dim(send_list, me, 0, keepdims=False)
    q = (j - nblocks) % slot
    srcof = jnp.where(j < nblocks, j, jnp.where(j < nblocks + slot, jnp.take(mine, q), q))
    return order, rowof, srcof.astype(jnp.int32)


def apply_operator(blocked, tile_vals, plan, send_list):
    order, rowof, srcof = plan
    nblocks = blocked.shape[0]
    nrows, slot = send_list.shape
    me = lax.axis_index("rows")
    pieces = []
    for shift in range(1, nrows):
        dest = (me + shift) % nrows
        wanted = lax.dynamic_index_in_dim(send_list, dest, 0, keepdims=False)
        chunk = jnp.take(blocked, wanted, axis=0)
        pairs = [(i, (i + shift) % nrows) for i in range(nrows)]
        pieces.append(lax.ppermute(chunk, "rows", pairs))
    own = run_tiles(order, rowof, srcof, [blocked], tile_vals, 0, [nblocks + slot], nblocks)
    received = run_tiles(
        order, rowof, srcof, pieces, tile_vals, nblocks + slot, [slot] * (nrows - 1), nblocks
    )
    return own + received


def tree_sum_rows(value, nrows):
    step = 1
    while step < nrows:
        pairs = [(i, i ^ step) for i in range(nrows)]
        value = value + lax.ppermute(value, "rows", pairs)
        step *= 2
    return value


def gather_cols(piece, ncols):
    half = 2 if ncols % 2 == 0 else 1
    outer = ncols // half
    me = lax.axis_index("cols")
    parts, owners = [piece], [me]
    for shift in range(1, outer):
        pairs = [(i, (i + shift * half) % ncols) for i in range(ncols)]
        parts.append(lax.ppermute(piece, "cols", pairs))
        owners.append((me - shift * half) % ncols)
    if half == 2:
        pairs = [(i, i ^ 1) for i in range(ncols)]
        count = len(parts)
        for n in range(count):
            parts.append(lax.ppermute(parts[n], "cols", pairs))
            owners.append(owners[n] ^ 1)
    return parts, owners


def body(vectors, tile_vals, tile_row, tile_src, send_list, ritz_matrix):
    columns, length = vectors.shape
    side = tile_vals.shape[1]
    nblocks = length // side
    nrows = lax.axis_size("rows")
    ncols = lax.axis_size("cols")
    plan = plan_slots(tile_row, tile_src, send_list)
    start = vectors.reshape(columns, nblocks, side).transpose(1, 0, 2)
    first_pass = apply_operator(start, tile_vals, plan, send_list).astype(jnp.bfloat16)
    second = apply_operator(first_pass, tile_vals, plan, send_list)
    filtered = (2.0 * second - start.astype(jnp.float32)).astype(jnp.bfloat16)
    total_nodes = length * nrows
    parts, owners = gather_cols(filtered, ncols)
    operated = apply_operator(filtered, tile_vals, plan, send_list).astype(jnp.bfloat16)
    contract = (((0, 2), (0, 2)), ((), ()))
    gram_cols = [lax.dot_general(filtered, p, contract, preferred_element_type=jnp.float32) for p in parts]
    proj_cols = [lax.dot_general(operated, p, contract, preferred_element_type=jnp.float32) for p in parts]
    owner_ids = jnp.stack(owners).astype(jnp.int32)
    place = jnp.zeros((ncols,), jnp.int32).at[owner_ids].set(jnp.arange(ncols, dtype=jnp.int32))
    gram_rel = jnp.stack(gram_cols)
    proj_rel = jnp.stack(proj_cols)
    both = jnp.stack([jnp.take(gram_rel, place, axis=0), jnp.take(proj_rel, place, axis=0)])
    both = both.transpose(0, 2, 1, 3).reshape(2, columns, ncols * columns)
    both = tree_sum_rows(both, nrows)
    gram_matrix = both[0] / total_nodes
    projected = both[1] / total_nodes
    ritz_rows = ritz_matrix.reshape(ncols, columns, ritz_matrix.shape[1])
    turned = None
    for p, owner in zip(parts, owners):
        weights = lax.dynamic_index_in_dim(ritz_rows, owner, 0, keepdims=False)
        term = jnp.einsum("ij,bic->jbc", weights, p, preferred_element_type=jnp.float32)
        turned = term if turned is None else turned + term
    rotated = turned.astype(jnp.bfloat16).reshape(ritz_matrix.shape[1], length)
    return (rotated, gram_matrix, projected)


def solution(mesh):
    return jax.shard_map(
        body,
        mesh=mesh,
        in_specs=(
            P("cols", "rows"),
            P("rows", None, None),
            P("rows", None),
            P("rows", None),
            P("rows", None),
            P(None, "cols"),
        ),
        out_specs=(P("cols", "rows"), P("cols", None), P("cols", None)),
        check_vma=False,
    )
```

time: 191 us -> 250 us (1.31)
  Pallas kernels: 0 us -> 130 us
  matrix products: 48.9 us -> 7.96 us
  waiting for transfers between devices: 26.6 us -> 11.2 us
  starting transfers between devices: 61.5 us -> 47.5 us
  local copies, waits for them, and re-layouts: 31.9 us -> 24.3 us
  other arithmetic: 19.8 us -> 25.9 us
    pallas_call x0 -> x6, Pallas kernels: none -> 130 us  [run_tiles(): pl.pallas_call(kernel, out_shape=jax.ShapeDtypeStruct((nblocks, columns,...]
    dot_general x9 -> x12, matrix products: 48.9 us -> 7.96 us  [the longest x4 4.19 us: body(): jnp.einsum('ij,bic->jbc', weights, p, preferred_element_type=jnp.float32)]
    ppermute x22 -> x23, starting transfers between devices: 57.1 us -> 40.5 us  [the longest x21 40.5 us: apply_operator(): pieces.append(lax.ppermute(chunk, 'rows', pairs))]
    ppermute x22 -> x23, waiting for transfers between devices: 18.5 us -> 7.95 us  [the longest x21 7.35 us: apply_operator(): pieces.append(lax.ppermute(chunk, 'rows', pairs))]
    select_n x26 -> x27, other arithmetic: 8.89 us -> 16.9 us  [the longest x1 6.34 us: plan_slots(): jnp.where(j < nblocks, j, jnp.where(j < nblocks + slot, jnp.take(mine, q)...]
    gather x28 -> x25, local copies, waits for them, and re-layouts: 24 us -> 16.2 us  [the longest x21 12.6 us: apply_operator(): chunk = jnp.take(blocked, wanted, axis=0)]
    ppermute x3, waiting for transfers between devices: 8.11 us -> 3.2 us  [tree_sum_rows(): value = value + lax.ppermute(value, 'rows', pairs)]
    convert_element_type x1 -> x3, other arithmetic: 0.09 us -> 4.71 us  [the longest x1 1.72 us: body(): apply_operator(filtered, tile_vals, plan, send_list).astype(jnp.bfloat16)]
  transfers between devices with their start and end apart: 26 -> 27, of which waited for: 8 -> 8; matrix products, arithmetic and copies ran while one was open for 19% -> 15% of each run, Pallas kernels for 0% -> 25%
where the time goes in v2:
time: 250 us; the launch traced here: 249 us
  Pallas kernels  130 us (52%)
  starting transfers between devices  47.5 us (19%)
  other arithmetic  25.9 us (10%)
  local copies, waits for them, and re-layouts  24.3 us (10%)
  waiting for transfers between devices  11.2 us (4%)
  matrix products  7.96 us (3%)
    pallas_call x6, Pallas kernels, run_tiles(): pl.pallas_call(kernel, out_shape=jax.ShapeDtypeStruct((nblocks, columns,...  130 us
    ppermute x21, starting transfers between devices, apply_operator(): pieces.append(lax.ppermute(chunk, 'rows', pairs))  40.5 us
    gather x21, local copies, waits for them, and re-layouts, apply_operator(): chunk = jnp.take(blocked, wanted, axis=0)  12.6 us
    ppermute x21, waiting for transfers between devices, apply_operator(): pieces.append(lax.ppermute(chunk, 'rows', pairs))  7.35 us
    select_n x1, other arithmetic, plan_slots(): jnp.where(j < nblocks, j, jnp.where(j < nblocks + slot, jnp.take(mine, q)...  6.34 us
    ppermute x3, starting transfers between devices, tree_sum_rows(): value = value + lax.ppermute(value, 'rows', pairs)  5.37 us
  transfers between devices with their start and end apart: 27, of which 8 were waited for; matrix products, arithmetic and copies ran while one was open for 15% of the time, Pallas kernels for 25%

profile of v2, /device:TPU:0, one launch (start us, length us, event | category | flops | bytes accessed | tf_op | source)
XLA Modules:
  0.0 248.7 jit_solution(7393375635267512805)
XLA Ops:
  3.6 6.1 %collective-permute-start.6 = (bf16[16,16,256]{2,1,0:T(8,128)(2,1)S(1)}, bf16[16,16,256]{2,1,0:T(8,128)(2,1)S(1)}, u32[]{:S(2)}, u32[]{:S(2)}) collective-permute-start(bf16[16,16,256]{2,1,0:T(8,128)(2,1)S(1)} %broadcast_select_fusion.2), channel_id=1, source_target_pairs={{0,28},{4,0},{8,4},{12,8},{16,12},{20,16},{24,20},{28,24},{1,29},{... | collective-permute-start | bytes 393224 | tf_op jit(solution)/shard_map/ppermute | solution.py:103
  12.2 3.0 %collective-permute-start.3 = (bf16[16,16,256]{2,1,0:T(8,128)(2,1)S(1)}, bf16[16,16,256]{2,1,0:T(8,128)(2,1)S(1)}, u32[]{:S(2)}, u32[]{:S(2)}) collective-permute-start(bf16[16,16,256]{2,1,0:T(8,128)(2,1)S(1)} %broadcast_select_fusion.11), channel_id=1, source_target_pairs={{0,16},{4,20},{8,24},{12,28},{16,0},{20,4},{24,8},{28,12},{1,17},{... | collective-permute-start | bytes 393224 | tf_op jit(solution)/shard_map/ppermute | solution.py:103
  18.7 5.0 %compare_select_fusion.1 = (s32[192,1]{0,1:T(1,128)S(1)}, s32[192,1]{0,1:T(1,128)S(1)}) fusion(s32[1,192]{1,0:T(1,128)} %param.13, s32[]{:T(128)S(6)} %axis_index.17, s32[]{:T(128)} %bitcast.20, s32[]{:T(128)} %bitcast.19, s32[]{:T(128)} %bitcast.18, s32[]{:T(128)} %bitcast.17, s32[]{:T(128)} %bitcast.16, s32[]{:T(128)} %bitcast.15, s32[]{:T(128)} %bitcast.14), kind=kLoop, calls=%fused_computation.74 | loop fusion | flops 12864 | bytes 2336 | tf_op jit(solution)/shard_map/select_n | solution.py:83
  25.0 1.6 gather_fusion
  28.0 6.3 %compare_select_fusion.30.src_ref = s32[192]{0:T(256)} fusion(pred[192]{0:T(512)(128)(4,1)S(1)} %get-tuple-element.57, pred[192]{0:T(512)(128)(4,1)S(1)} %get-tuple-element.58, pred[192]{0:T(512)(128)(4,1)S(1)} %get-tuple-element.59, pred[192]{0:T(512)(128)(4,1)S(1)} %get-tuple-element.60, pred[192]{0:T(512)(128)(4,1)S(1)} %get-tuple-element.61, ...), kind=kLoop, calls=%fused_computation.152 | loop fusion | flops 6144 | bytes 3300 | tf_op jit(solution)/shard_map/jit(_where)/select_n | solution.py:88
  34.4 18.6 %shard_map.85 = f32[64,16,256]{2,1,0:T(8,128)} custom-call(s32[192]{0:T(256)} %copy-done.29, s32[192]{0:T(256)} %and_select_fusion.6.row_ref, s32[192]{0:T(256)} %compare_select_fusion.30.src_ref, bf16[64,16,256]{2,1,0:T(8,128)(2,1)} %bitcast.165, bf16[192,256,256]{2,1,0:T(8,128)(2,1)} %refs_7_.5), custom_call_target="tpu_custom_call" | custom-call | tf_op jit(solution)/shard_map/pallas_call | solution.py:57
  53.5 1.8 collective-permute-start.1
  57.1 4.1 %collective-permute-done.1.refs_1_ = bf16[16,16,256]{2,1,0:T(8,128)(2,1)S(1)} collective-permute-done((bf16[16,16,256]{2,1,0:T(8,128)(2,1)S(1)}, bf16[16,16,256]{2,1,0:T(8,128)(2,1)S(1)}, u32[]{:S(2)}, u32[]{:S(2)}) %collective-permute-start.1) | collective-permute-done | bytes 131104 | tf_op jit(solution)/shard_map/ppermute | solution.py:103
  61.2 2.0 collective-permute-done.refs_0_
  63.9 24.7 %shard_map.86 = f32[64,16,256]{2,1,0:T(8,128)} custom-call(s32[192]{0:T(256)} %copy-done.29, s32[192]{0:T(256)} %and_select_fusion.6.row_ref, s32[192]{0:T(256)} %compare_select_fusion.30.src_ref, bf16[16,16,256]{2,1,0:T(8,128)(2,1)} %copy-done.28, bf16[16,16,256]{2,1,0:T(8,128)(2,1)} %copy-done.27, bf16[16,16,256]{2,1,0:T(8,128)(2,1)} %copy-done.12, ...), custom_call_target="tpu_custom_call" | custom-call | tf_op jit(solution)/shard_map/pallas_call | solution.py:57
  94.8 1.7 collective-permute-start.12
  97.6 2.8 %collective-permute-start.10 = (bf16[16,16,256]{2,1,0:T(8,128)(2,1)S(1)}, bf16[16,16,256]{2,1,0:T(8,128)(2,1)S(1)}, u32[]{:S(2)}, u32[]{:S(2)}) collective-permute-start(bf16[16,16,256]{2,1,0:T(8,128)(2,1)S(1)} %broadcast_select_fusion.10), channel_id=1, source_target_pairs={{0,16},{4,20},{8,24},{12,28},{16,0},{20,4},{24,8},{28,12},{1,17},{... | collective-permute-start | bytes 393224 | tf_op jit(solution)/shard_map/ppermute | solution.py:103
  102.1 1.7 collective-permute-start.8
  103.8 2.0 collective-permute-start.7
  107.8 18.7 %shard_map.87 = f32[64,16,256]{2,1,0:T(8,128)} custom-call(s32[192]{0:T(256)} %copy-done.29, s32[192]{0:T(256)} %and_select_fusion.6.row_ref, s32[192]{0:T(256)} %compare_select_fusion.30.src_ref, bf16[64,16,256]{2,1,0:T(8,128)(2,1)} %copy-done.3, bf16[192,256,256]{2,1,0:T(8,128)(2,1)} %refs_7_.5), custom_call_target="tpu_custom_call" | custom-call | tf_op jit(solution)/shard_map/pallas_call | solution.py:57
  128.0 24.7 %shard_map.88 = f32[64,16,256]{2,1,0:T(8,128)} custom-call(s32[192]{0:T(256)} %copy-done.29, s32[192]{0:T(256)} %and_select_fusion.6.row_ref, s32[192]{0:T(256)} %compare_select_fusion.30.src_ref, bf16[16,16,256]{2,1,0:T(8,128)(2,1)} %copy-done.22, bf16[16,16,256]{2,1,0:T(8,128)(2,1)} %copy-done.20, bf16[16,16,256]{2,1,0:T(8,128)(2,1)} %copy-done.17, ...), custom_call_target="tpu_custom_call" | custom-call | tf_op jit(solution)/shard_map/pallas_call | solution.py:57
  159.1 18.6 %shard_map.89 = f32[64,16,256]{2,1,0:T(8,128)} custom-call(s32[192]{0:T(256)} %copy-done.29, s32[192]{0:T(256)} %and_select_fusion.6.row_ref, s32[192]{0:T(256)} %compare_select_fusion.30.src_ref, bf16[64,16,256]{2,1,0:T(8,128)(2,1)} %copy-done.1, bf16[192,256,256]{2,1,0:T(8,128)(2,1)} %refs_7_.5), custom_call_target="tpu_custom_call" | custom-call | tf_op jit(solution)/shard_map/pallas_call | solution.py:57
  177.8 9.7 %collective-permute-start.17 = (bf16[16,16,256]{2,1,0:T(8,128)(2,1)S(1)}, bf16[16,16,256]{2,1,0:T(8,128)(2,1)S(1)}, u32[]{:S(2)}, u32[]{:S(2)}) collective-permute-start(bf16[16,16,256]{2,1,0:T(8,128)(2,1)S(1)} %broadcast_select_fusion.18), channel_id=1, source_target_pairs={{0,4},{4,8},{8,12},{12,16},{16,20},{20,24},{24,28},{28,0},{1,5},{5... | collective-permute-start | bytes 393224 | tf_op jit(solution)/shard_map/ppermute | solution.py:103
  187.9 3.9 %collective-permute-start.20 = (bf16[16,16,256]{2,1,0:T(8,128)(2,1)S(1)}, bf16[16,16,256]{2,1,0:T(8,128)(2,1)S(1)}, u32[]{:S(2)}, u32[]{:S(2)}) collective-permute-start(bf16[16,16,256]{2,1,0:T(8,128)(2,1)S(1)} %broadcast_select_fusion.9), channel_id=1, source_target_pairs={{0,16},{4,20},{8,24},{12,28},{16,0},{20,4},{24,8},{28,12},{1,17},{... | collective-permute-start | bytes 393224 | tf_op jit(solution)/shard_map/ppermute | solution.py:103
  194.7 3.8 %collective-permute-start.22 = (bf16[16,16,256]{2,1,0:T(8,128)(2,1)S(1)}, bf16[16,16,256]{2,1,0:T(8,128)(2,1)S(1)}, u32[]{:S(2)}, u32[]{:S(2)}) collective-permute-start(bf16[16,16,256]{2,1,0:T(8,128)(2,1)S(1)} %broadcast_select_fusion.3), channel_id=1, source_target_pairs={{0,24},{4,28},{8,0},{12,4},{16,8},{20,12},{24,16},{28,20},{1,25},{... | collective-permute-start | bytes 393224 | tf_op jit(solution)/shard_map/ppermute | solution.py:103
  204.2 24.7 %shard_map.90 = f32[64,16,256]{2,1,0:T(8,128)} custom-call(s32[192]{0:T(256)} %copy-done.29, s32[192]{0:T(256)} %and_select_fusion.6.row_ref, s32[192]{0:T(256)} %compare_select_fusion.30.src_ref, bf16[16,16,256]{2,1,0:T(8,128)(2,1)} %copy-done.18, bf16[16,16,256]{2,1,0:T(8,128)(2,1)} %copy-done.19, bf16[16,16,256]{2,1,0:T(8,128)(2,1)} %copy-done.21, ...), custom_call_target="tpu_custom_call" | custom-call | tf_op jit(solution)/shard_map/pallas_call | solution.py:57
  228.9 1.7 add_convert_fusion
  235.8 2.2 collective-permute-start.24
  243.4 1.9 collective-permute-start.26
  (234 shorter events, 55.4 us)
Async XLA Ops:
  3.6 49.9 %collective-permute-start.6 = (bf16[16,16,256]{2,1,0:T(8,128)(2,1)S(1)}, bf16[16,16,256]{2,1,0:T(8,128)(2,1)S(1)}, u32[]{:S(2)}, u32[]{:S(2)}) collective-permute-start(bf16[16,16,256]{2,1,0:T(8,128)(2,1)S(1)} %broadcast_select_fusion.2), channel_id=1, source_target_pairs={{0,28},{4,0},{8,4},{12,8},{16,12},{20,16},{24,20},{28,24},{1,29},{... | collective-permute-start | bytes 393224 | tf_op jit(solution)/shard_map/ppermute | solution.py:103
  10.3 45.0 %collective-permute-start.5 = (bf16[16,16,256]{2,1,0:T(8,128)(2,1)S(1)}, bf16[16,16,256]{2,1,0:T(8,128)(2,1)S(1)}, u32[]{:S(2)}, u32[]{:S(2)}) collective-permute-start(bf16[16,16,256]{2,1,0:T(8,128)(2,1)S(1)} %broadcast_select_fusion.5), channel_id=1, source_target_pairs={{0,24},{4,28},{8,0},{12,4},{16,8},{20,12},{24,16},{28,20},{1,25},{... | collective-permute-start | bytes 393224 | tf_op jit(solution)/shard_map/ppermute | solution.py:103
  11.5 45.6 %collective-permute-start.4 = (bf16[16,16,256]{2,1,0:T(8,128)(2,1)S(1)}, bf16[16,16,256]{2,1,0:T(8,128)(2,1)S(1)}, u32[]{:S(2)}, u32[]{:S(2)}) collective-permute-start(bf16[16,16,256]{2,1,0:T(8,128)(2,1)S(1)} %broadcast_select_fusion.8), channel_id=1, source_target_pairs={{0,20},{4,24},{8,28},{12,0},{16,4},{20,8},{24,12},{28,16},{1,21},{... | collective-permute-start | bytes 393224 | tf_op jit(solution)/shard_map/ppermute | solution.py:103
  12.2 44.8 %collective-permute-start.3 = (bf16[16,16,256]{2,1,0:T(8,128)(2,1)S(1)}, bf16[16,16,256]{2,1,0:T(8,128)(2,1)S(1)}, u32[]{:S(2)}, u32[]{:S(2)}) collective-permute-start(bf16[16,16,256]{2,1,0:T(8,128)(2,1)S(1)} %broadcast_select_fusion.11), channel_id=1, source_target_pairs={{0,16},{4,20},{8,24},{12,28},{16,0},{20,4},{24,8},{28,12},{1,17},{... | collective-permute-start | bytes 393224 | tf_op jit(solution)/shard_map/ppermute | solution.py:103
  15.9 41.1 %collective-permute-start.2 = (bf16[16,16,256]{2,1,0:T(8,128)(2,1)S(1)}, bf16[16,16,256]{2,1,0:T(8,128)(2,1)S(1)}, u32[]{:S(2)}, u32[]{:S(2)}) collective-permute-start(bf16[16,16,256]{2,1,0:T(8,128)(2,1)S(1)} %broadcast_select_fusion.14), channel_id=1, source_target_pairs={{0,12},{4,16},{8,20},{12,24},{16,28},{20,0},{24,4},{28,8},{1,13},{... | collective-permute-start | bytes 393224 | tf_op jit(solution)/shard_map/ppermute | solution.py:103
  53.5 7.7 %collective-permute-start.1 = (bf16[16,16,256]{2,1,0:T(8,128)(2,1)S(1)}, bf16[16,16,256]{2,1,0:T(8,128)(2,1)S(1)}, u32[]{:S(2)}, u32[]{:S(2)}) collective-permute-start(bf16[16,16,256]{2,1,0:T(8,128)(2,1)S(1)} %broadcast_select_fusion.17), channel_id=1, source_target_pairs={{0,8},{4,12},{8,16},{12,20},{16,24},{20,28},{24,0},{28,4},{1,9},{5... | collective-permute-start | bytes 393224 | tf_op jit(solution)/shard_map/ppermute | solution.py:103
  55.3 7.8 %collective-permute-start = (bf16[16,16,256]{2,1,0:T(8,128)(2,1)S(1)}, bf16[16,16,256]{2,1,0:T(8,128)(2,1)S(1)}, u32[]{:S(2)}, u32[]{:S(2)}) collective-permute-start(bf16[16,16,256]{2,1,0:T(8,128)(2,1)S(1)} %broadcast_select_fusion.20), channel_id=1, source_target_pairs={{0,4},{4,8},{8,12},{12,16},{16,20},{20,24},{24,28},{28,0},{1,5},{5... | collective-permute-start | bytes 393224 | tf_op jit(solution)/shard_map/ppermute | solution.py:103
  94.2 7.9 %collective-permute-start.13 = (bf16[16,16,256]{2,1,0:T(8,128)(2,1)S(1)}, bf16[16,16,256]{2,1,0:T(8,128)(2,1)S(1)}, u32[]{:S(2)}, u32[]{:S(2)}) collective-permute-start(bf16[16,16,256]{2,1,0:T(8,128)(2,1)S(1)} %broadcast_select_fusion.1), channel_id=1, source_target_pairs={{0,28},{4,0},{8,4},{12,8},{16,12},{20,16},{24,20},{28,24},{1,29},{... | collective-permute-start | bytes 393224 | tf_op jit(solution)/shard_map/ppermute | solution.py:103
  94.8 9.0 %collective-permute-start.12 = (bf16[16,16,256]{2,1,0:T(8,128)(2,1)S(1)}, bf16[16,16,256]{2,1,0:T(8,128)(2,1)S(1)}, u32[]{:S(2)}, u32[]{:S(2)}) collective-permute-start(bf16[16,16,256]{2,1,0:T(8,128)(2,1)S(1)} %broadcast_select_fusion.4), channel_id=1, source_target_pairs={{0,24},{4,28},{8,0},{12,4},{16,8},{20,12},{24,16},{28,20},{1,25},{... | collective-permute-start | bytes 393224 | tf_op jit(solution)/shard_map/ppermute | solution.py:103
  96.6 29.9 %collective-permute-start.11 = (bf16[16,16,256]{2,1,0:T(8,128)(2,1)S(1)}, bf16[16,16,256]{2,1,0:T(8,128)(2,1)S(1)}, u32[]{:S(2)}, u32[]{:S(2)}) collective-permute-start(bf16[16,16,256]{2,1,0:T(8,128)(2,1)S(1)} %broadcast_select_fusion.7), channel_id=1, source_target_pairs={{0,20},{4,24},{8,28},{12,0},{16,4},{20,8},{24,12},{28,16},{1,21},{... | collective-permute-start | bytes 393224 | tf_op jit(solution)/shard_map/ppermute | solution.py:103
  97.6 28.9 %collective-permute-start.10 = (bf16[16,16,256]{2,1,0:T(8,128)(2,1)S(1)}, bf16[16,16,256]{2,1,0:T(8,128)(2,1)S(1)}, u32[]{:S(2)}, u32[]{:S(2)}) collective-permute-start(bf16[16,16,256]{2,1,0:T(8,128)(2,1)S(1)} %broadcast_select_fusion.10), channel_id=1, source_target_pairs={{0,16},{4,20},{8,24},{12,28},{16,0},{20,4},{24,8},{28,12},{1,17},{... | collective-permute-start | bytes 393224 | tf_op jit(solution)/shard_map/ppermute | solution.py:103
  100.5 26.1 %collective-permute-start.9 = (bf16[16,16,256]{2,1,0:T(8,128)(2,1)S(1)}, bf16[16,16,256]{2,1,0:T(8,128)(2,1)S(1)}, u32[]{:S(2)}, u32[]{:S(2)}) collective-permute-start(bf16[16,16,256]{2,1,0:T(8,128)(2,1)S(1)} %broadcast_select_fusion.13), channel_id=1, source_target_pairs={{0,12},{4,16},{8,20},{12,24},{16,28},{20,0},{24,4},{28,8},{1,13},{... | collective-permute-start | bytes 393224 | tf_op jit(solution)/shard_map/ppermute | solution.py:103
  102.1 24.5 %collective-permute-start.8 = (bf16[16,16,256]{2,1,0:T(8,128)(2,1)}, bf16[16,16,256]{2,1,0:T(8,128)(2,1)S(1)}, u32[]{:S(2)}, u32[]{:S(2)}) collective-permute-start(bf16[16,16,256]{2,1,0:T(8,128)(2,1)} %broadcast_select_fusion.16), channel_id=1, source_target_pairs={{0,8},{4,12},{8,16},{12,20},{16,24},{20,28},{24,0},{28,4},{1,9},{5... | collective-permute-start | bytes 393224 | tf_op jit(solution)/shard_map/ppermute | solution.py:103
  103.8 22.8 %collective-permute-start.7 = (bf16[16,16,256]{2,1,0:T(8,128)(2,1)S(1)}, bf16[16,16,256]{2,1,0:T(8,128)(2,1)S(1)}, u32[]{:S(2)}, u32[]{:S(2)}) collective-permute-start(bf16[16,16,256]{2,1,0:T(8,128)(2,1)S(1)} %broadcast_select_fusion.19), channel_id=1, source_target_pairs={{0,4},{4,8},{8,12},{12,16},{16,20},{20,24},{24,28},{28,0},{1,5},{5... | collective-permute-start | bytes 393224 | tf_op jit(solution)/shard_map/ppermute | solution.py:103
  177.8 16.9 %collective-permute-start.17 = (bf16[16,16,256]{2,1,0:T(8,128)(2,1)S(1)}, bf16[16,16,256]{2,1,0:T(8,128)(2,1)S(1)}, u32[]{:S(2)}, u32[]{:S(2)}) collective-permute-start(bf16[16,16,256]{2,1,0:T(8,128)(2,1)S(1)} %broadcast_select_fusion.18), channel_id=1, source_target_pairs={{0,4},{4,8},{8,12},{12,16},{16,20},{20,24},{24,28},{28,0},{1,5},{5... | collective-permute-start | bytes 393224 | tf_op jit(solution)/shard_map/ppermute | solution.py:103
  187.5 11.0 %collective-permute-start.18 = (bf16[16,16,256]{2,1,0:T(8,128)(2,1)S(1)}, bf16[16,16,256]{2,1,0:T(8,128)(2,1)S(1)}, u32[]{:S(2)}, u32[]{:S(2)}) collective-permute-start(bf16[16,16,256]{2,1,0:T(8,128)(2,1)S(1)} %broadcast_select_fusion.15), channel_id=1, source_target_pairs={{0,8},{4,12},{8,16},{12,20},{16,24},{20,28},{24,0},{28,4},{1,9},{5... | collective-permute-start | bytes 393224 | tf_op jit(solution)/shard_map/ppermute | solution.py:103
  187.7 12.9 %collective-permute-start.19 = (bf16[16,16,256]{2,1,0:T(8,128)(2,1)S(1)}, bf16[16,16,256]{2,1,0:T(8,128)(2,1)S(1)}, u32[]{:S(2)}, u32[]{:S(2)}) collective-permute-start(bf16[16,16,256]{2,1,0:T(8,128)(2,1)S(1)} %broadcast_select_fusion.12), channel_id=1, source_target_pairs={{0,12},{4,16},{8,20},{12,24},{16,28},{20,0},{24,4},{28,8},{1,13},{... | collective-permute-start | bytes 393224 | tf_op jit(solution)/shard_map/ppermute | solution.py:103
  187.9 14.4 %collective-permute-start.20 = (bf16[16,16,256]{2,1,0:T(8,128)(2,1)S(1)}, bf16[16,16,256]{2,1,0:T(8,128)(2,1)S(1)}, u32[]{:S(2)}, u32[]{:S(2)}) collective-permute-start(bf16[16,16,256]{2,1,0:T(8,128)(2,1)S(1)} %broadcast_select_fusion.9), channel_id=1, source_target_pairs={{0,16},{4,20},{8,24},{12,28},{16,0},{20,4},{24,8},{28,12},{1,17},{... | collective-permute-start | bytes 393224 | tf_op jit(solution)/shard_map/ppermute | solution.py:103
  192.4 9.8 %collective-permute-start.21 = (bf16[16,16,256]{2,1,0:T(8,128)(2,1)S(1)}, bf16[16,16,256]{2,1,0:T(8,128)(2,1)S(1)}, u32[]{:S(2)}, u32[]{:S(2)}) collective-permute-start(bf16[16,16,256]{2,1,0:T(8,128)(2,1)S(1)} %broadcast_select_fusion.6), channel_id=1, source_target_pairs={{0,20},{4,24},{8,28},{12,0},{16,4},{20,8},{24,12},{28,16},{1,21},{... | collective-permute-start | bytes 393224 | tf_op jit(solution)/shard_map/ppermute | solution.py:103
  194.7 8.1 %collective-permute-start.22 = (bf16[16,16,256]{2,1,0:T(8,128)(2,1)S(1)}, bf16[16,16,256]{2,1,0:T(8,128)(2,1)S(1)}, u32[]{:S(2)}, u32[]{:S(2)}) collective-permute-start(bf16[16,16,256]{2,1,0:T(8,128)(2,1)S(1)} %broadcast_select_fusion.3), channel_id=1, source_target_pairs={{0,24},{4,28},{8,0},{12,4},{16,8},{20,12},{24,16},{28,20},{1,25},{... | collective-permute-start | bytes 393224 | tf_op jit(solution)/shard_map/ppermute | solution.py:103
  198.5 5.0 %collective-permute-start.23 = (bf16[16,16,256]{2,1,0:T(8,128)(2,1)S(1)}, bf16[16,16,256]{2,1,0:T(8,128)(2,1)S(1)}, u32[]{:S(2)}, u32[]{:S(2)}) collective-permute-start(bf16[16,16,256]{2,1,0:T(8,128)(2,1)S(1)} %broadcast_select_fusion), channel_id=1, source_target_pairs={{0,28},{4,0},{8,4},{12,8},{16,12},{20,16},{24,20},{28,24},{1,29},{... | collective-permute-start | bytes 393224 | tf_op jit(solution)/shard_map/ppermute | solution.py:103
  200.7 30.3 %collective-permute-start.14 = (bf16[64,16,256]{2,1,0:T(8,128)(2,1)}, bf16[64,16,256]{2,1,0:T(8,128)(2,1)S(1)}, u32[]{:S(2)}, u32[]{:S(2)}) collective-permute-start(bf16[64,16,256]{2,1,0:T(8,128)(2,1)} %copy-done.1), channel_id=1, source_target_pairs={{0,2},{1,3},{2,0},{3,1},{4,6},{5,7},{6,4},{7,5},{8,10},{9,11},{10,... | collective-permute-start | bytes 1572872 | tf_op jit(solution)/shard_map/ppermute | solution.py:127
  202.3 29.4 %collective-permute-start.15 = (bf16[64,16,256]{2,1,0:T(8,128)(2,1)}, bf16[64,16,256]{2,1,0:T(8,128)(2,1)S(1)}, u32[]{:S(2)}, u32[]{:S(2)}) collective-permute-start(bf16[64,16,256]{2,1,0:T(8,128)(2,1)} %copy-done.1), channel_id=1, source_target_pairs={{0,1},{1,0},{2,3},{3,2},{4,5},{5,4},{6,7},{7,6},{8,9},{9,8},{10,11... | collective-permute-start | bytes 1572872 | tf_op jit(solution)/shard_map/ppermute | solution.py:133
  243.4 4.6 %collective-permute-start.26 = (f32[2,16,64]{2,1,0:T(8,128)S(1)}, f32[2,16,64]{2,1,0:T(8,128)S(1)}, u32[]{:S(2)}, u32[]{:S(2)}) collective-permute-start(f32[2,16,64]{2,1,0:T(8,128)S(1)} %add.342), channel_id=1, source_target_pairs={{0,16},{4,20},{8,24},{12,28},{16,0},{20,4},{24,8},{28,12},{1,17},{... | collective-permute-start | bytes 24584 | tf_op jit(solution)/shard_map/ppermute | solution.py:115
  (51 other events, 1783.7 us)

commit v3 on v2

--- a/solution.py
+++ b/solution.py
@@ -1,74 +1,7 @@
-import functools
-
 import jax
 import jax.numpy as jnp
 from jax import lax
-from jax.experimental import pallas as pl
-from jax.experimental.pallas import tpu as pltpu
 from jax.sharding import PartitionSpec as P
-
-NBUF = 8
-
-
-def tile_kernel(order_ref, row_ref, src_ref, *refs, first, counts):
-    nsrc = len(counts)
-    sources = refs[:nsrc]
-    tiles_hbm = refs[nsrc]
-    out_ref = refs[nsrc + 1]
-    buf = refs[nsrc + 2]
-    sem = refs[nsrc + 3]
-    total = sum(counts)
-    out_ref[...] = jnp.zeros(out_ref.shape, out_ref.dtype)
-
-    def copy(j, slot):
-        return pltpu.make_async_copy(tiles_hbm.at[order_ref[first + j]], buf.at[slot], sem.at[slot])
-
-    for j in range(min(NBUF, total)):
-        copy(j, j).start()
-    base = 0
-    for k, cnt in enumerate(counts):
-
-        def step(q, carry, k=k, base=base):
-            j = base + q
-            slot = j % NBUF
-            copy(j, slot).wait()
-            lhs = sources[k][src_ref[first + j]]
-            prod = lax.dot_general(
-                lhs, buf[slot], (((1,), (1,)), ((), ())), preferred_element_type=jnp.float32
-            )
-            r = row_ref[first + j]
-            out_ref[r] = out_ref[r] + prod
-
-            @pl.when(j + NBUF < total)
-            def _():
-                copy(j + NBUF, slot).start()
-
-            return carry
-
-        lax.fori_loop(0, cnt, step, 0)
-        base += cnt
-
-
-def run_tiles(order, rowof, srcof, sources, tile_vals, first, counts, nblocks):
-    columns, side = sources[0].shape[1], sources[0].shape[2]
-    kernel = functools.partial(tile_kernel, first=first, counts=tuple(counts))
-    in_specs = [pl.BlockSpec(memory_space=pltpu.VMEM) for _ in sources]
-    in_specs.append(pl.BlockSpec(memory_space=pl.ANY))
-    return pl.pallas_call(
-        kernel,
-        out_shape=jax.ShapeDtypeStruct((nblocks, columns, side), jnp.float32),
-        grid_spec=pltpu.PrefetchScalarGridSpec(
-            num_scalar_prefetch=3,
-            grid=(1,),
-            in_specs=in_specs,
-            out_specs=pl.BlockSpec(memory_space=pltpu.VMEM),
-            scratch_shapes=[
-                pltpu.VMEM((NBUF,) + tile_vals.shape[1:], tile_vals.dtype),
-                pltpu.SemaphoreType.DMA((NBUF,)),
-            ],
-        ),
-    )(order, rowof, srcof, *sources, tile_vals)
-
 
 def plan_slots(tile_row, tile_src, send_list):
     nrows, slot = send_list.shape
@@ -89,10 +22,8 @@
     return order, rowof, srcof.astype(jnp.int32)
 
 
-def apply_operator(blocked, tile_vals, plan, send_list):
-    order, rowof, srcof = plan
-    nblocks = blocked.shape[0]
-    nrows, slot = send_list.shape
+def exchange(blocked, send_list):
+    nrows = send_list.shape[0]
     me = lax.axis_index("rows")
     pieces = []
     for shift in range(1, nrows):
@@ -101,11 +32,40 @@
         chunk = jnp.take(blocked, wanted, axis=0)
         pairs = [(i, (i + shift) % nrows) for i in range(nrows)]
         pieces.append(lax.ppermute(chunk, "rows", pairs))
-    own = run_tiles(order, rowof, srcof, [blocked], tile_vals, 0, [nblocks + slot], nblocks)
-    received = run_tiles(
-        order, rowof, srcof, pieces, tile_vals, nblocks + slot, [slot] * (nrows - 1), nblocks
-    )
-    return own + received
+    mine = lax.dynamic_index_in_dim(send_list, me, 0, keepdims=False)
+    return jnp.take(blocked, mine, axis=0), pieces
+
+
+def row_sum(onehot, products):
+    return jnp.einsum("bj,jkr->bkr", onehot, products, precision=lax.Precision.HIGHEST)
+
+
+def products_of(sources, tiles):
+    return jnp.einsum("jkc,jrc->jkr", sources, tiles, preferred_element_type=jnp.float32)
+
+
+def first_apply(blocked, tile_vals, plan, send_list):
+    order, rowof, _ = plan
+    nblocks = blocked.shape[0]
+    own_self, pieces = exchange(blocked, send_list)
+    sources = jnp.concatenate([blocked, own_self] + pieces, axis=0)
+    slot_of_tile = jnp.zeros_like(order).at[order].set(jnp.arange(order.shape[0], dtype=order.dtype))
+    chosen = jnp.take(sources, slot_of_tile, axis=0)
+    products = products_of(chosen, tile_vals)
+    rows = jnp.take(rowof, slot_of_tile)
+    onehot = (rows[None, :] == jnp.arange(nblocks, dtype=jnp.int32)[:, None]).astype(jnp.float32)
+    return row_sum(onehot, products)
+
+
+def sorted_apply(blocked, tiles_sorted, onehot, send_list):
+    nblocks = blocked.shape[0]
+    slot = send_list.shape[1]
+    own_self, pieces = exchange(blocked, send_list)
+    split = nblocks + slot
+    own = products_of(jnp.concatenate([blocked, own_self], axis=0), tiles_sorted[:split])
+    out = row_sum(onehot[:, :split], own)
+    received = products_of(jnp.concatenate(pieces, axis=0), tiles_sorted[split:])
+    return out + row_sum(onehot[:, split:], received)
 
 
 def tree_sum_rows(value, nrows):
@@ -143,12 +103,15 @@
     ncols = lax.axis_size("cols")
     plan = plan_slots(tile_row, tile_src, send_list)
     start = vectors.reshape(columns, nblocks, side).transpose(1, 0, 2)
-    first_pass = apply_operator(start, tile_vals, plan, send_list).astype(jnp.bfloat16)
-    second = apply_operator(first_pass, tile_vals, plan, send_list)
+    first_pass = first_apply(start, tile_vals, plan, send_list).astype(jnp.bfloat16)
+    order, rowof, _ = plan
+    tiles_sorted = jnp.take(tile_vals, order, axis=0)
+    onehot = (rowof[None, :] == jnp.arange(nblocks, dtype=jnp.int32)[:, None]).astype(jnp.float32)
+    second = sorted_apply(first_pass, tiles_sorted, onehot, send_list)
     filtered = (2.0 * second - start.astype(jnp.float32)).astype(jnp.bfloat16)
     total_nodes = length * nrows
     parts, owners = gather_cols(filtered, ncols)
-    operated = apply_operator(filtered, tile_vals, plan, send_list).astype(jnp.bfloat16)
+    operated = sorted_apply(filtered, tiles_sorted, onehot, send_list).astype(jnp.bfloat16)
     contract = (((0, 2), (0, 2)), ((), ()))
     gram_cols = [lax.dot_general(filtered, p, contract, preferred_element_type=jnp.float32) for p in parts]
     proj_cols = [lax.dot_general(operated, p, contract, preferred_element_type=jnp.float32) for p in parts]

time: 250 us -> 204 us (0.82)
  Pallas kernels: 130 us -> 0 us
  matrix products: 7.96 us -> 57.5 us
  local copies, waits for them, and re-layouts: 24.3 us -> 49.9 us
  waiting for transfers between devices: 11.2 us -> 21 us
    pallas_call x6 -> x0, Pallas kernels: 130 us -> none  [run_tiles(): pl.pallas_call(kernel, out_shape=jax.ShapeDtypeStruct((nblocks, columns,...]
    dot_general x0 -> x10, matrix products: none -> 50.3 us  [the longest x5 40.1 us: products_of(): jnp.einsum('jkc,jrc->jkr', sources, tiles, preferred_element_type=jnp.flo...]
    gather x22 -> x27, local copies, waits for them, and re-layouts: 13.3 us -> 36.4 us  [the longest x1 19.4 us: body(): tiles_sorted = jnp.take(tile_vals, order, axis=0)]
    select_n x22 -> x25, other arithmetic: 10.7 us -> 26.4 us  [the longest x1 21.2 us: body(): tiles_sorted = jnp.take(tile_vals, order, axis=0)]
    ppermute x21, waiting for transfers between devices: 7.35 us -> 13.3 us  [exchange(): pieces.append(lax.ppermute(chunk, 'rows', pairs))]
    select_n x1, other arithmetic: 4.99 us -> 0.03 us  [plan_slots(): jnp.zeros((ntiles,), jnp.int32).at[slots]]
    convert_element_type x3 -> x0, other arithmetic: 4.71 us -> none  [the longest x1 1.72 us: body(): apply_operator(filtered, tile_vals, plan, send_list).astype(jnp.bfloat16)]
    ppermute x3, waiting for transfers between devices: 3.2 us -> 7.76 us  [tree_sum_rows(): value = value + lax.ppermute(value, 'rows', pairs)]
  transfers between devices with their start and end apart: 27 -> 27, of which waited for: 8 -> 7; matrix products, arithmetic and copies ran while one was open for 15% -> 45% of each run, Pallas kernels for 25% -> 0%
where the time goes in v3:
time: 204 us; the launch traced here: 203 us
  matrix products  57.5 us (28%)
  local copies, waits for them, and re-layouts  49.9 us (24%)
  starting transfers between devices  45.4 us (22%)
  other arithmetic  27.5 us (13%)
  waiting for transfers between devices  21 us (10%)
    ppermute x21, starting transfers between devices, exchange(): pieces.append(lax.ppermute(chunk, 'rows', pairs))  41.5 us
    dot_general x5, matrix products, products_of(): jnp.einsum('jkc,jrc->jkr', sources, tiles, preferred_element_type=jnp.flo...  40.1 us
    select_n x1, other arithmetic, body(): tiles_sorted = jnp.take(tile_vals, order, axis=0)  21.2 us
    gather x1, local copies, waits for them, and re-layouts, body(): tiles_sorted = jnp.take(tile_vals, order, axis=0)  19.4 us
    ppermute x21, waiting for transfers between devices, exchange(): pieces.append(lax.ppermute(chunk, 'rows', pairs))  13.3 us
    gather x21, local copies, waits for them, and re-layouts, exchange(): chunk = jnp.take(blocked, wanted, axis=0)  11.7 us
    dot_general x5, matrix products, row_sum(): jnp.einsum('bj,jkr->bkr', onehot, products, precision=lax.Precision.HIGHEST)  10.3 us
    ppermute x3, waiting for transfers between devices, tree_sum_rows(): value = value + lax.ppermute(value, 'rows', pairs)  7.76 us
  transfers between devices with their start and end apart: 27, of which 7 were waited for; matrix products, arithmetic and copies ran while one was open for 45% of the time, Pallas kernels for 0%

profile of v3, /device:TPU:0, one launch (start us, length us, event | category | flops | bytes accessed | tf_op | source)
XLA Modules:
  0.0 203.2 jit_solution(11457652304716290917)
XLA Ops:
  3.6 3.0 %collective-permute-start = (bf16[16,16,256]{2,0,1:T(8,128)(2,1)}, bf16[16,16,256]{2,0,1:T(8,128)(2,1)S(1)}, u32[]{:S(2)}, u32[]{:S(2)}) collective-permute-start(bf16[16,16,256]{2,0,1:T(8,128)(2,1)} %copy_select_fusion.8), channel_id=1, source_target_pairs={{0,4},{4,8},{8,12},{12,16},{16,20},{20,24},{24,28},{28,0},{1,5},{5... | collective-permute-start | bytes 393224 | tf_op jit(solution)/shard_map/ppermute | solution.py:34
  10.8 2.6 %collective-permute-start.2 = (bf16[16,16,256]{2,0,1:T(8,128)(2,1)}, bf16[16,16,256]{2,0,1:T(8,128)(2,1)}, u32[]{:S(2)}, u32[]{:S(2)}) collective-permute-start(bf16[16,16,256]{2,0,1:T(8,128)(2,1)} %copy_select_fusion.6), channel_id=1, source_target_pairs={{0,12},{4,16},{8,20},{12,24},{16,28},{20,0},{24,4},{28,8},{1,13},{... | collective-permute-start | bytes 393224 | tf_op jit(solution)/shard_map/ppermute | solution.py:34
  17.2 2.6 %collective-permute-start.4 = (bf16[16,16,256]{2,0,1:T(8,128)(2,1)}, bf16[16,16,256]{2,0,1:T(8,128)(2,1)}, u32[]{:S(2)}, u32[]{:S(2)}) collective-permute-start(bf16[16,16,256]{2,0,1:T(8,128)(2,1)} %copy_select_fusion.4), channel_id=1, source_target_pairs={{0,20},{4,24},{8,28},{12,0},{16,4},{20,8},{24,12},{28,16},{1,21},{... | collective-permute-start | bytes 393224 | tf_op jit(solution)/shard_map/ppermute | solution.py:34
  28.2 19.4 %gather_fusion.1 = bf16[192,256,256]{2,1,0:T(8,128)(2,1)} fusion(bf16[192,256,256]{2,1,0:T(8,128)(2,1)} %param.13, s32[1024]{0:T(1024)S(1)} %pad_clamp_fusion.10), kind=kCustom, calls=%fused_computation.29 | custom fusion | bytes 50332416 | tf_op jit(solution)/shard_map/jit(_take)/gather | solution.py:108
  47.8 21.2 %broadcast_select_fusion = bf16[192,256,256]{2,1,0:T(8,128)(2,1)} fusion(bf16[192,256,256]{2,1,0:T(8,128)(2,1)} %gather_fusion.1, pred[192]{0:T(512)(128)(4,1)S(1)} %get-tuple-element.9), kind=kLoop, calls=%fused_computation.33 | loop fusion | flops 12582912 | bytes 50331840 | tf_op jit(solution)/shard_map/jit(_take)/select_n | solution.py:108
  78.7 12.0 %fusion.14 = f32[192,16,256]{2,1,0:T(8,128)S(1)} fusion(bf16[192,256,256]{2,1,0:T(8,128)(2,1)} %param.13, bf16[192,16,256]{2,1,0:T(8,128)(2,1)} %gather_fusion, pred[192]{0:T(512)(128)(4,1)S(1)} %get-tuple-element.7), kind=kOutput, calls=%fused_computation.48 | convolution fusion | flops 403439616 | bytes 29884608 | tf_op jit(solution)/shard_map/jkc,jrc->jkr/dot_general | solution.py:44
  90.7 3.2 %fusion.39 = bf16[64,16,256]{2,0,1:T(8,128)(2,1)S(1)} fusion(f32[192,16,256]{2,1,0:T(8,128)S(1)} %fusion.14, s32[192]{0:T(256)S(1)} %get-tuple-element.6), kind=kOutput, calls=%fused_computation.64 | convolution fusion | flops 604254208 | bytes 3670784 | tf_op jit(solution)/shard_map/bj,jkr->bkr/dot_general | solution.py:40
  101.8 2.1 %collective-permute-start.9 = (bf16[16,16,256]{2,1,0:T(8,128)(2,1)S(1)}, bf16[16,16,256]{2,1,0:T(8,128)(2,1)S(1)}, u32[]{:S(2)}, u32[]{:S(2)}) collective-permute-start(bf16[16,16,256]{2,1,0:T(8,128)(2,1)S(1)} %broadcast_select_fusion.10), channel_id=1, source_target_pairs={{0,12},{4,16},{8,20},{12,24},{16,28},{20,0},{24,4},{28,8},{1,13},{... | collective-permute-start | bytes 393224 | tf_op jit(solution)/shard_map/ppermute | solution.py:34
  103.9 2.2 %collective-permute-start.10 = (bf16[16,16,256]{2,1,0:T(8,128)(2,1)S(1)}, bf16[16,16,256]{2,1,0:T(8,128)(2,1)S(1)}, u32[]{:S(2)}, u32[]{:S(2)}) collective-permute-start(bf16[16,16,256]{2,1,0:T(8,128)(2,1)S(1)} %broadcast_select_fusion.8), channel_id=1, source_target_pairs={{0,16},{4,20},{8,24},{12,28},{16,0},{20,4},{24,8},{28,12},{1,17},{... | collective-permute-start | bytes 393224 | tf_op jit(solution)/shard_map/ppermute | solution.py:34
  106.2 3.2 %collective-permute-start.11 = (bf16[16,16,256]{2,1,0:T(8,128)(2,1)S(1)}, bf16[16,16,256]{2,1,0:T(8,128)(2,1)S(1)}, u32[]{:S(2)}, u32[]{:S(2)}) collective-permute-start(bf16[16,16,256]{2,1,0:T(8,128)(2,1)S(1)} %broadcast_select_fusion.6), channel_id=1, source_target_pairs={{0,20},{4,24},{8,28},{12,0},{16,4},{20,8},{24,12},{28,16},{1,21},{... | collective-permute-start | bytes 393224 | tf_op jit(solution)/shard_map/ppermute | solution.py:34
  109.6 6.8 %fusion.6 = f32[80,16,256]{2,1,0:T(8,128)S(1)} fusion(bf16[192,256,256]{2,1,0:T(8,128)(2,1)} %broadcast_select_fusion, bf16[80,16,256]{2,0,1:T(8,128)(2,1)S(1)} %pad_maximum_fusion), kind=kOutput, calls=%fused_computation.40 | convolution fusion | flops 167772160 | bytes 12451840 | tf_op jit(solution)/shard_map/jkc,jrc->jkr/dot_general | solution.py:44
  119.9 3.9 %collective-permute-done.12 = bf16[16,16,256]{2,1,0:T(8,128)(2,1)S(1)} collective-permute-done((bf16[16,16,256]{2,1,0:T(8,128)(2,1)S(1)}, bf16[16,16,256]{2,1,0:T(8,128)(2,1)S(1)}, u32[]{:S(2)}, u32[]{:S(2)}) %collective-permute-start.12) | collective-permute-done | bytes 131104 | tf_op jit(solution)/shard_map/ppermute | solution.py:34
  123.9 7.2 %fusion.2 = f32[112,16,256]{2,1,0:T(8,128)S(1)} fusion(bf16[112,16,256]{2,1,0:T(8,128)(2,1)S(1)} %constant_dynamic-update-slice_fusion.8, bf16[192,256,256]{2,1,0:T(8,128)(2,1)} %broadcast_select_fusion), kind=kOutput, calls=%fused_computation.36 | convolution fusion | flops 234881024 | bytes 17432576 | tf_op jit(solution)/shard_map/jkc,jrc->jkr/dot_general | solution.py:44
  131.1 2.1 %fusion.36 = bf16[64,16,256]{2,0,1:T(8,128)(2,1)S(1)} fusion(f32[64,16,256]{2,0,1:T(8,128)S(1)} %fusion.31, f32[112,16,256]{2,1,0:T(8,128)S(1)} %fusion.2, pred[64,192]{1,0:T(32,128)(4,1)S(1)} %iota_compare_fusion.1, bf16[16,64,256]{2,1,0:T(8,128)(2,1)S(1)} %bitcast.137), kind=kOutput, calls=%fused_computation.63 | convolution fusion | flops 353632256 | bytes 3940352 | tf_op jit(solution)/shard_map/bj,jkr->bkr/dot_general | solution.py:40
  140.2 2.9 %collective-permute-start.17 = (bf16[16,16,256]{2,1,0:T(8,128)(2,1)S(1)}, bf16[16,16,256]{2,1,0:T(8,128)(2,1)S(1)}, u32[]{:S(2)}, u32[]{:S(2)}) collective-permute-start(bf16[16,16,256]{2,1,0:T(8,128)(2,1)S(1)} %broadcast_select_fusion.13), channel_id=1, source_target_pairs={{0,4},{4,8},{8,12},{12,16},{16,20},{20,24},{24,28},{28,0},{1,5},{5... | collective-permute-start | bytes 393224 | tf_op jit(solution)/shard_map/ppermute | solution.py:34
  144.4 6.8 %fusion.4 = f32[80,16,256]{2,1,0:T(8,128)S(1)} fusion(bf16[192,256,256]{2,1,0:T(8,128)(2,1)} %broadcast_select_fusion, bf16[80,16,256]{2,0,1:T(8,128)(2,1)S(1)} %pad_maximum_fusion.1), kind=kOutput, calls=%fused_computation.38 | convolution fusion | flops 167772160 | bytes 12451840 | tf_op jit(solution)/shard_map/jkc,jrc->jkr/dot_general | solution.py:44
  153.2 3.4 %collective-permute-start.20 = (bf16[16,16,256]{2,1,0:T(8,128)(2,1)S(1)}, bf16[16,16,256]{2,1,0:T(8,128)(2,1)S(1)}, u32[]{:S(2)}, u32[]{:S(2)}) collective-permute-start(bf16[16,16,256]{2,1,0:T(8,128)(2,1)S(1)} %broadcast_select_fusion.7), channel_id=1, source_target_pairs={{0,16},{4,20},{8,24},{12,28},{16,0},{20,4},{24,8},{28,12},{1,17},{... | collective-permute-start | bytes 393224 | tf_op jit(solution)/shard_map/ppermute | solution.py:34
  160.5 6.1 %collective-permute-done.20 = bf16[16,16,256]{2,1,0:T(8,128)(2,1)S(1)} collective-permute-done((bf16[16,16,256]{2,1,0:T(8,128)(2,1)S(1)}, bf16[16,16,256]{2,1,0:T(8,128)(2,1)S(1)}, u32[]{:S(2)}, u32[]{:S(2)}) %collective-permute-start.20) | collective-permute-done | bytes 131104 | tf_op jit(solution)/shard_map/ppermute | solution.py:34
  166.6 5.5 %collective-permute-start.23 = (bf16[16,16,256]{2,1,0:T(8,128)(2,1)S(1)}, bf16[16,16,256]{2,1,0:T(8,128)(2,1)S(1)}, u32[]{:S(2)}, u32[]{:S(2)}) collective-permute-start(bf16[16,16,256]{2,1,0:T(8,128)(2,1)S(1)} %broadcast_select_fusion.1), channel_id=1, source_target_pairs={{0,28},{4,0},{8,4},{12,8},{16,12},{20,16},{24,20},{28,24},{1,29},{... | collective-permute-start | bytes 393224 | tf_op jit(solution)/shard_map/ppermute | solution.py:34
  172.1 2.5 %collective-permute-done.23 = bf16[16,16,256]{2,1,0:T(8,128)(2,1)S(1)} collective-permute-done((bf16[16,16,256]{2,1,0:T(8,128)(2,1)S(1)}, bf16[16,16,256]{2,1,0:T(8,128)(2,1)S(1)}, u32[]{:S(2)}, u32[]{:S(2)}) %collective-permute-start.23) | collective-permute-done | bytes 131104 | tf_op jit(solution)/shard_map/ppermute | solution.py:34
  174.7 7.2 %fusion = f32[112,16,256]{2,1,0:T(8,128)S(1)} fusion(bf16[112,16,256]{2,1,0:T(8,128)(2,1)S(1)} %constant_dynamic-update-slice_fusion.15, bf16[192,256,256]{2,1,0:T(8,128)(2,1)} %broadcast_select_fusion), kind=kOutput, calls=%fused_computation.34 | convolution fusion | flops 234881024 | bytes 17432576 | tf_op jit(solution)/shard_map/jkc,jrc->jkr/dot_general | solution.py:44
  190.9 3.3 %collective-permute-done.24 = f32[2,16,64]{2,1,0:T(8,128)S(1)} collective-permute-done((f32[2,16,64]{2,1,0:T(8,128)S(1)}, f32[2,16,64]{2,1,0:T(8,128)S(1)}, u32[]{:S(2)}, u32[]{:S(2)}) %collective-permute-start.24) | collective-permute-done | bytes 8224 | tf_op jit(solution)/shard_map/ppermute | solution.py:75
  194.6 3.3 %collective-permute-done.25 = f32[2,16,64]{2,1,0:T(8,128)S(1)} collective-permute-done((f32[2,16,64]{2,1,0:T(8,128)S(1)}, f32[2,16,64]{2,1,0:T(8,128)S(1)}, u32[]{:S(2)}, u32[]{:S(2)}) %collective-permute-start.25) | collective-permute-done | bytes 8224 | tf_op jit(solution)/shard_map/ppermute | solution.py:75
  198.0 2.3 %collective-permute-start.26 = (f32[2,16,64]{2,1,0:T(8,128)S(1)}, f32[2,16,64]{2,1,0:T(8,128)S(1)}, u32[]{:S(2)}, u32[]{:S(2)}) collective-permute-start(f32[2,16,64]{2,1,0:T(8,128)S(1)} %add.299), channel_id=1, source_target_pairs={{0,16},{4,20},{8,24},{12,28},{16,0},{20,4},{24,8},{28,12},{1,17},{... | collective-permute-start | bytes 24584 | tf_op jit(solution)/shard_map/ppermute | solution.py:75
  (193 shorter events, 66.8 us)
Async XLA Ops:
  3.6 65.5 %collective-permute-start = (bf16[16,16,256]{2,0,1:T(8,128)(2,1)}, bf16[16,16,256]{2,0,1:T(8,128)(2,1)S(1)}, u32[]{:S(2)}, u32[]{:S(2)}) collective-permute-start(bf16[16,16,256]{2,0,1:T(8,128)(2,1)} %copy_select_fusion.8), channel_id=1, source_target_pairs={{0,4},{4,8},{8,12},{12,16},{16,20},{20,24},{24,28},{28,0},{1,5},{5... | collective-permute-start | bytes 393224 | tf_op jit(solution)/shard_map/ppermute | solution.py:34
  7.9 62.7 %collective-permute-start.1 = (bf16[16,16,256]{2,0,1:T(8,128)(2,1)}, bf16[16,16,256]{2,0,1:T(8,128)(2,1)S(1)}, u32[]{:S(2)}, u32[]{:S(2)}) collective-permute-start(bf16[16,16,256]{2,0,1:T(8,128)(2,1)} %copy_select_fusion.7), channel_id=1, source_target_pairs={{0,8},{4,12},{8,16},{12,20},{16,24},{20,28},{24,0},{28,4},{1,9},{5... | collective-permute-start | bytes 393224 | tf_op jit(solution)/shard_map/ppermute | solution.py:34
  10.8 61.5 %collective-permute-start.2 = (bf16[16,16,256]{2,0,1:T(8,128)(2,1)}, bf16[16,16,256]{2,0,1:T(8,128)(2,1)}, u32[]{:S(2)}, u32[]{:S(2)}) collective-permute-start(bf16[16,16,256]{2,0,1:T(8,128)(2,1)} %copy_select_fusion.6), channel_id=1, source_target_pairs={{0,12},{4,16},{8,20},{12,24},{16,28},{20,0},{24,4},{28,8},{1,13},{... | collective-permute-start | bytes 393224 | tf_op jit(solution)/shard_map/ppermute | solution.py:34
  14.7 58.5 %collective-permute-start.3 = (bf16[16,16,256]{2,0,1:T(8,128)(2,1)}, bf16[16,16,256]{2,0,1:T(8,128)(2,1)}, u32[]{:S(2)}, u32[]{:S(2)}) collective-permute-start(bf16[16,16,256]{2,0,1:T(8,128)(2,1)} %copy_select_fusion.5), channel_id=1, source_target_pairs={{0,16},{4,20},{8,24},{12,28},{16,0},{20,4},{24,8},{28,12},{1,17},{... | collective-permute-start | bytes 393224 | tf_op jit(solution)/shard_map/ppermute | solution.py:34
  17.2 56.9 %collective-permute-start.4 = (bf16[16,16,256]{2,0,1:T(8,128)(2,1)}, bf16[16,16,256]{2,0,1:T(8,128)(2,1)}, u32[]{:S(2)}, u32[]{:S(2)}) collective-permute-start(bf16[16,16,256]{2,0,1:T(8,128)(2,1)} %copy_select_fusion.4), channel_id=1, source_target_pairs={{0,20},{4,24},{8,28},{12,0},{16,4},{20,8},{24,12},{28,16},{1,21},{... | collective-permute-start | bytes 393224 | tf_op jit(solution)/shard_map/ppermute | solution.py:34
  69.1 5.9 %collective-permute-start.5 = (bf16[16,16,256]{2,0,1:T(8,128)(2,1)S(1)}, bf16[16,16,256]{2,0,1:T(8,128)(2,1)S(1)}, u32[]{:S(2)}, u32[]{:S(2)}) collective-permute-start(bf16[16,16,256]{2,0,1:T(8,128)(2,1)S(1)} %copy_select_fusion.3), channel_id=1, source_target_pairs={{0,24},{4,28},{8,0},{12,4},{16,8},{20,12},{24,16},{28,20},{1,25},{... | collective-permute-start | bytes 393224 | tf_op jit(solution)/shard_map/ppermute | solution.py:34
  70.6 5.2 %collective-permute-start.6 = (bf16[16,16,256]{2,0,1:T(8,128)(2,1)S(1)}, bf16[16,16,256]{2,0,1:T(8,128)(2,1)S(1)}, u32[]{:S(2)}, u32[]{:S(2)}) collective-permute-start(bf16[16,16,256]{2,0,1:T(8,128)(2,1)S(1)} %copy_select_fusion.2), channel_id=1, source_target_pairs={{0,28},{4,0},{8,4},{12,8},{16,12},{20,16},{24,20},{28,24},{1,29},{... | collective-permute-start | bytes 393224 | tf_op jit(solution)/shard_map/ppermute | solution.py:34
  99.6 18.4 %collective-permute-start.7 = (bf16[16,16,256]{2,1,0:T(8,128)(2,1)S(1)}, bf16[16,16,256]{2,1,0:T(8,128)(2,1)S(1)}, u32[]{:S(2)}, u32[]{:S(2)}) collective-permute-start(bf16[16,16,256]{2,1,0:T(8,128)(2,1)S(1)} %broadcast_select_fusion.14), channel_id=1, source_target_pairs={{0,4},{4,8},{8,12},{12,16},{16,20},{20,24},{24,28},{28,0},{1,5},{5... | collective-permute-start | bytes 393224 | tf_op jit(solution)/shard_map/ppermute | solution.py:34
  101.3 16.9 %collective-permute-start.8 = (bf16[16,16,256]{2,1,0:T(8,128)(2,1)S(1)}, bf16[16,16,256]{2,1,0:T(8,128)(2,1)S(1)}, u32[]{:S(2)}, u32[]{:S(2)}) collective-permute-start(bf16[16,16,256]{2,1,0:T(8,128)(2,1)S(1)} %broadcast_select_fusion.12), channel_id=1, source_target_pairs={{0,8},{4,12},{8,16},{12,20},{16,24},{20,28},{24,0},{28,4},{1,9},{5... | collective-permute-start | bytes 393224 | tf_op jit(solution)/shard_map/ppermute | solution.py:34
  101.8 18.1 %collective-permute-start.9 = (bf16[16,16,256]{2,1,0:T(8,128)(2,1)S(1)}, bf16[16,16,256]{2,1,0:T(8,128)(2,1)S(1)}, u32[]{:S(2)}, u32[]{:S(2)}) collective-permute-start(bf16[16,16,256]{2,1,0:T(8,128)(2,1)S(1)} %broadcast_select_fusion.10), channel_id=1, source_target_pairs={{0,12},{4,16},{8,20},{12,24},{16,28},{20,0},{24,4},{28,8},{1,13},{... | collective-permute-start | bytes 393224 | tf_op jit(solution)/shard_map/ppermute | solution.py:34
  103.9 16.0 %collective-permute-start.10 = (bf16[16,16,256]{2,1,0:T(8,128)(2,1)S(1)}, bf16[16,16,256]{2,1,0:T(8,128)(2,1)S(1)}, u32[]{:S(2)}, u32[]{:S(2)}) collective-permute-start(bf16[16,16,256]{2,1,0:T(8,128)(2,1)S(1)} %broadcast_select_fusion.8), channel_id=1, source_target_pairs={{0,16},{4,20},{8,24},{12,28},{16,0},{20,4},{24,8},{28,12},{1,17},{... | collective-permute-start | bytes 393224 | tf_op jit(solution)/shard_map/ppermute | solution.py:34
  106.2 13.7 %collective-permute-start.11 = (bf16[16,16,256]{2,1,0:T(8,128)(2,1)S(1)}, bf16[16,16,256]{2,1,0:T(8,128)(2,1)S(1)}, u32[]{:S(2)}, u32[]{:S(2)}) collective-permute-start(bf16[16,16,256]{2,1,0:T(8,128)(2,1)S(1)} %broadcast_select_fusion.6), channel_id=1, source_target_pairs={{0,20},{4,24},{8,28},{12,0},{16,4},{20,8},{24,12},{28,16},{1,21},{... | collective-permute-start | bytes 393224 | tf_op jit(solution)/shard_map/ppermute | solution.py:34
  118.0 5.8 %collective-permute-start.12 = (bf16[16,16,256]{2,1,0:T(8,128)(2,1)S(1)}, bf16[16,16,256]{2,1,0:T(8,128)(2,1)S(1)}, u32[]{:S(2)}, u32[]{:S(2)}) collective-permute-start(bf16[16,16,256]{2,1,0:T(8,128)(2,1)S(1)} %broadcast_select_fusion.4), channel_id=1, source_target_pairs={{0,24},{4,28},{8,0},{12,4},{16,8},{20,12},{24,16},{28,20},{1,25},{... | collective-permute-start | bytes 393224 | tf_op jit(solution)/shard_map/ppermute | solution.py:34
  118.2 5.6 %collective-permute-start.13 = (bf16[16,16,256]{2,1,0:T(8,128)(2,1)S(1)}, bf16[16,16,256]{2,1,0:T(8,128)(2,1)S(1)}, u32[]{:S(2)}, u32[]{:S(2)}) collective-permute-start(bf16[16,16,256]{2,1,0:T(8,128)(2,1)S(1)} %broadcast_select_fusion.2), channel_id=1, source_target_pairs={{0,28},{4,0},{8,4},{12,8},{16,12},{20,16},{24,20},{28,24},{1,29},{... | collective-permute-start | bytes 393224 | tf_op jit(solution)/shard_map/ppermute | solution.py:34
  138.1 46.5 %collective-permute-start.14 = (bf16[64,16,256]{2,0,1:T(8,128)(2,1)S(1)}, bf16[64,16,256]{2,0,1:T(8,128)(2,1)S(1)}, u32[]{:S(2)}, u32[]{:S(2)}) collective-permute-start(bf16[64,16,256]{2,0,1:T(8,128)(2,1)S(1)} %fusion.36), channel_id=1, source_target_pairs={{0,2},{1,3},{2,0},{3,1},{4,6},{5,7},{6,4},{7,5},{8,10},{9,11},{10,... | collective-permute-start | bytes 1572872 | tf_op jit(solution)/shard_map/ppermute | solution.py:87
  139.6 46.4 %collective-permute-start.15 = (bf16[64,16,256]{2,0,1:T(8,128)(2,1)S(1)}, bf16[64,16,256]{2,0,1:T(8,128)(2,1)S(1)}, u32[]{:S(2)}, u32[]{:S(2)}) collective-permute-start(bf16[64,16,256]{2,0,1:T(8,128)(2,1)S(1)} %fusion.36), channel_id=1, source_target_pairs={{0,1},{1,0},{2,3},{3,2},{4,5},{5,4},{6,7},{7,6},{8,9},{9,8},{10,11... | collective-permute-start | bytes 1572872 | tf_op jit(solution)/shard_map/ppermute | solution.py:93
  140.2 13.1 %collective-permute-start.17 = (bf16[16,16,256]{2,1,0:T(8,128)(2,1)S(1)}, bf16[16,16,256]{2,1,0:T(8,128)(2,1)S(1)}, u32[]{:S(2)}, u32[]{:S(2)}) collective-permute-start(bf16[16,16,256]{2,1,0:T(8,128)(2,1)S(1)} %broadcast_select_fusion.13), channel_id=1, source_target_pairs={{0,4},{4,8},{8,12},{12,16},{16,20},{20,24},{24,28},{28,0},{1,5},{5... | collective-permute-start | bytes 393224 | tf_op jit(solution)/shard_map/ppermute | solution.py:34
  143.1 13.5 %collective-permute-start.18 = (bf16[16,16,256]{2,1,0:T(8,128)(2,1)S(1)}, bf16[16,16,256]{2,1,0:T(8,128)(2,1)S(1)}, u32[]{:S(2)}, u32[]{:S(2)}) collective-permute-start(bf16[16,16,256]{2,1,0:T(8,128)(2,1)S(1)} %broadcast_select_fusion.11), channel_id=1, source_target_pairs={{0,8},{4,12},{8,16},{12,20},{16,24},{20,28},{24,0},{28,4},{1,9},{5... | collective-permute-start | bytes 393224 | tf_op jit(solution)/shard_map/ppermute | solution.py:34
  143.9 14.6 %collective-permute-start.19 = (bf16[16,16,256]{2,1,0:T(8,128)(2,1)S(1)}, bf16[16,16,256]{2,1,0:T(8,128)(2,1)S(1)}, u32[]{:S(2)}, u32[]{:S(2)}) collective-permute-start(bf16[16,16,256]{2,1,0:T(8,128)(2,1)S(1)} %broadcast_select_fusion.9), channel_id=1, source_target_pairs={{0,12},{4,16},{8,20},{12,24},{16,28},{20,0},{24,4},{28,8},{1,13},{... | collective-permute-start | bytes 393224 | tf_op jit(solution)/shard_map/ppermute | solution.py:34
  153.2 13.4 %collective-permute-start.20 = (bf16[16,16,256]{2,1,0:T(8,128)(2,1)S(1)}, bf16[16,16,256]{2,1,0:T(8,128)(2,1)S(1)}, u32[]{:S(2)}, u32[]{:S(2)}) collective-permute-start(bf16[16,16,256]{2,1,0:T(8,128)(2,1)S(1)} %broadcast_select_fusion.7), channel_id=1, source_target_pairs={{0,16},{4,20},{8,24},{12,28},{16,0},{20,4},{24,8},{28,12},{1,17},{... | collective-permute-start | bytes 393224 | tf_op jit(solution)/shard_map/ppermute | solution.py:34
  156.6 15.4 %collective-permute-start.21 = (bf16[16,16,256]{2,1,0:T(8,128)(2,1)S(1)}, bf16[16,16,256]{2,1,0:T(8,128)(2,1)S(1)}, u32[]{:S(2)}, u32[]{:S(2)}) collective-permute-start(bf16[16,16,256]{2,1,0:T(8,128)(2,1)S(1)} %broadcast_select_fusion.5), channel_id=1, source_target_pairs={{0,20},{4,24},{8,28},{12,0},{16,4},{20,8},{24,12},{28,16},{1,21},{... | collective-permute-start | bytes 393224 | tf_op jit(solution)/shard_map/ppermute | solution.py:34
  158.5 13.6 %collective-permute-start.22 = (bf16[16,16,256]{2,1,0:T(8,128)(2,1)S(1)}, bf16[16,16,256]{2,1,0:T(8,128)(2,1)S(1)}, u32[]{:S(2)}, u32[]{:S(2)}) collective-permute-start(bf16[16,16,256]{2,1,0:T(8,128)(2,1)S(1)} %broadcast_select_fusion.3), channel_id=1, source_target_pairs={{0,24},{4,28},{8,0},{12,4},{16,8},{20,12},{24,16},{28,20},{1,25},{... | collective-permute-start | bytes 393224 | tf_op jit(solution)/shard_map/ppermute | solution.py:34
  166.6 8.1 %collective-permute-start.23 = (bf16[16,16,256]{2,1,0:T(8,128)(2,1)S(1)}, bf16[16,16,256]{2,1,0:T(8,128)(2,1)S(1)}, u32[]{:S(2)}, u32[]{:S(2)}) collective-permute-start(bf16[16,16,256]{2,1,0:T(8,128)(2,1)S(1)} %broadcast_select_fusion.1), channel_id=1, source_target_pairs={{0,28},{4,0},{8,4},{12,8},{16,12},{20,16},{24,20},{28,24},{1,29},{... | collective-permute-start | bytes 393224 | tf_op jit(solution)/shard_map/ppermute | solution.py:34
  198.0 4.6 %collective-permute-start.26 = (f32[2,16,64]{2,1,0:T(8,128)S(1)}, f32[2,16,64]{2,1,0:T(8,128)S(1)}, u32[]{:S(2)}, u32[]{:S(2)}) collective-permute-start(f32[2,16,64]{2,1,0:T(8,128)S(1)} %add.299), channel_id=1, source_target_pairs={{0,16},{4,20},{8,24},{12,28},{16,0},{20,4},{24,8},{28,12},{1,17},{... | collective-permute-start | bytes 24584 | tf_op jit(solution)/shard_map/ppermute | solution.py:75
  (12 other events, 111.1 us)
